TPU v7x, 32 devices: a whole 2x2x4 slice. The times are simulated.
32 devices in a mesh: row: 8 (over z, y), col: 4 (over x, core).
Axes of the slice: x: 2, y: 2, z: 4, core: 2. Of those that a mesh axis runs over, the one named last changes fastest.
Arguments:
- features: bfloat16 [4, 8192, 128], P('col', 'row'), may hold values from -6 to 6
- w_self: bfloat16 [128, 256], replicated, may hold values from -0.5 to 0.5
- w_neigh: bfloat16 [128, 256], replicated, may hold values from -2 to 2
- bias: float32 [256], replicated, may hold values from -3 to 3
- blocks: bfloat16 [8, 4, 320, 128, 128], P('row', 'col')
- blk_row: int32 [8, 4, 320], P('row', 'col'), may hold values from 0 to 31
- blk_slot: int32 [8, 4, 320], P('row', 'col'), may hold values from 0 to 15, as said below
- counts: int32 [8, 4, 1], P('row', 'col'), may hold values from 16 to 320, as said below
- col_list: int32 [8, 4, 8, 2], P('row', 'col'), may hold values from 0 to 7, as said below
- cotangent: bfloat16 [4, 8192, 256], P('col', 'row'), may hold values from -6 to 6
Outputs:
- output: bfloat16 [4, 8192, 256], P('col', 'row')
- grad_feats: bfloat16 [4, 8192, 128], P('col', 'row')
- grad_self: float32 [128, 256], replicated
- grad_neigh: float32 [128, 256], replicated
- grad_bias: float32 [256], replicated
Inputs may be any that keep to these rules, and one draw needn't show every extreme that they name: `col_list`: for each tile and owner the 2 entries are distinct. `blk_slot`: the first 16 slots of each tile name every read block once, in some order. `counts`: some tile has all 320 slots live.
All inputs are finite; a program needn't handle non-finite values.
Results may differ from a plain program's by a relative error of at most 0.0059.
Values may be sent and summed in bfloat16 or wider, within the bound.
No kernel may reach another device: no remote copies, remote signals or barrier semaphores. Data moves between devices by JAX's collectives and lax.ppermute only.
A program may use at most 128 MiB of HBM per device.

v0:
```python
import math

import jax
import jax.numpy as jnp
from jax import lax
from jax.sharding import PartitionSpec as P


def gelu_tanh(values):
    return jax.nn.gelu(values, approximate=True)


def select_rows(indices, table, total):
    picker = (indices[:, None] == jnp.arange(total, dtype=jnp.int32)[None, :]).astype(table.dtype)
    flat = table.reshape(total, -1)
    taken = jnp.dot(picker, flat, preferred_element_type=jnp.float32).astype(table.dtype)
    return taken.reshape((indices.shape[0],) + table.shape[1:])


def group_rows(indices, values, total):
    grouper = (jnp.arange(total, dtype=jnp.int32)[:, None] == indices[None, :]).astype(jnp.float32)
    flat = values.reshape(values.shape[0], -1)
    added = jnp.dot(
        grouper, flat, precision=lax.Precision.HIGHEST, preferred_element_type=jnp.float32
    )
    return added.reshape((total,) + values.shape[1:])


def on_device(
    features, w_self, w_neigh, bias, blocks, blk_row, blk_slot, counts, col_list, cotangent
):
    own_feats = features[0]
    node_count, feat_width = own_feats.shape
    block_size = blocks.shape[-1]
    slot_total = blocks.shape[2]
    owned_count = node_count // block_size
    row_count = lax.axis_size("row")
    col_count = lax.axis_size("col")
    picks_each = col_list.shape[-1]
    panel_blocks = col_count * node_count // block_size
    wanted = col_list[0, 0]
    asked_for = lax.all_to_all(wanted, "row", split_axis=0, concat_axis=0, tiled=True)
    live_mask = (jnp.arange(slot_total) < counts[0, 0, 0]).astype(jnp.bfloat16)
    adjacency = blocks[0, 0] * live_mask[:, None, None]
    block_rows = blk_row[0, 0]
    block_slots = blk_slot[0, 0]
    own_blocks = own_feats.reshape(owned_count, block_size, feat_width)
    outgoing = select_rows(asked_for.reshape(-1), own_blocks, owned_count)
    outgoing = outgoing.reshape(row_count, picks_each, block_size, feat_width)
    arrived = lax.all_to_all(outgoing, "row", split_axis=0, concat_axis=0, tiled=True)
    fetched = arrived.reshape(row_count * picks_each, block_size, feat_width)
    gathered = select_rows(block_slots, fetched, row_count * picks_each)
    products = jnp.einsum("kij,kjd->kid", adjacency, gathered, preferred_element_type=jnp.float32)
    partial_sums = group_rows(block_rows, products, panel_blocks)
    partial_sums = partial_sums.reshape(col_count * node_count, feat_width)
    row_weight = jnp.sum(adjacency, axis=2, dtype=jnp.float32)
    partial_degree = group_rows(block_rows, row_weight, panel_blocks).reshape(
        col_count * node_count
    )
    summed, degree = (
        lax.psum_scatter(partial_sums, "col", scatter_dimension=0, tiled=True),
        lax.psum_scatter(partial_degree, "col", scatter_dimension=0, tiled=True),
    )
    divisor = 1.0 + degree
    neighbors = (summed / divisor[:, None]).astype(jnp.bfloat16)
    hidden = (
        jnp.dot(own_feats, w_self, preferred_element_type=jnp.float32)
        + jnp.dot(neighbors, w_neigh, preferred_element_type=jnp.float32)
        + bias
    )
    output, pullback = jax.vjp(gelu_tanh, hidden)
    grad_hidden = pullback(cotangent[0].astype(jnp.float32))[0]
    grad_round = grad_hidden.astype(jnp.bfloat16)
    local_self = jnp.einsum("nd,nh->dh", own_feats, grad_round, preferred_element_type=jnp.float32)
    local_neigh = jnp.einsum("nd,nh->dh", neighbors, grad_round, preferred_element_type=jnp.float32)
    local_bias = jnp.sum(grad_round.astype(jnp.float32), axis=0)
    grad_self, grad_neigh, grad_bias = lax.psum(
        (local_self, local_neigh, local_bias), ("row", "col")
    )
    factor = 1.0 / math.sqrt(node_count * row_count * col_count)
    grad_agg = (
        jnp.einsum("nh,dh->nd", grad_round, w_neigh, preferred_element_type=jnp.float32)
        / divisor[:, None]
    )
    grad_agg = grad_agg.astype(jnp.bfloat16)
    adjoint_panel = lax.all_gather(grad_agg, "col", axis=0, tiled=True)
    row_pieces = select_rows(
        block_rows, adjoint_panel.reshape(panel_blocks, block_size, feat_width), panel_blocks
    )
    backward = jnp.einsum("kij,kid->kjd", adjacency, row_pieces, preferred_element_type=jnp.float32)
    per_slot = group_rows(block_slots, backward, row_count * picks_each)
    per_slot = per_slot.reshape(row_count, picks_each, block_size, feat_width)
    returned = lax.all_to_all(per_slot, "row", split_axis=0, concat_axis=0, tiled=True)
    incoming = group_rows(
        asked_for.reshape(-1),
        returned.reshape(row_count * picks_each, block_size, feat_width),
        owned_count,
    )
    incoming = incoming.reshape(node_count, feat_width)
    grad_feats = (
        jnp.einsum("nh,dh->nd", grad_round, w_self, preferred_element_type=jnp.float32) + incoming
    )
    return (
        output.astype(jnp.bfloat16)[None],
        grad_feats.astype(jnp.bfloat16)[None],
        grad_self * factor,
        grad_neigh * factor,
        grad_bias * factor,
    )


def solution(mesh):
    return jax.shard_map(
        on_device,
        mesh=mesh,
        in_specs=(
            P("col", "row", None),
            P(),
            P(),
            P(),
            P("row", "col", None, None, None),
            P("row", "col", None),
            P("row", "col", None),
            P("row", "col", None),
            P("row", "col", None, None),
            P("col", "row", None),
        ),
        out_specs=(P("col", "row", None), P("col", "row", None), P(), P(), P()),
        check_vma=False,
    )
```

profile of v0, /device:TPU:0, one launch (start us, length us, event | category | flops | bytes accessed | tf_op | source)
XLA Modules:
  0.0 363.4 jit_solution(15975753795149766940)
XLA Ops:
  7.2 1.4 copy.27
  8.6 7.3 %all-to-all-start = ((s32[8,1,2]{2,1,0:T(1,128)}), s32[8,1,2]{2,1,0:T(1,128)S(1)}, u32[]{:S(2)}, u32[]{:S(2)}) async-start(s32[8,1,2]{2,1,0:T(1,128)} %copy.27), calls=%async_computation | async-start | bytes 8192 | tf_op jit(solution)/shard_map/all_to_all | solution.py:42
  15.9 1.1 reshape_reshape_squeeze.3
  16.9 5.4 %all-to-all-done = s32[8,1,2]{2,1,0:T(1,128)S(1)} async-done(((s32[8,1,2]{2,1,0:T(1,128)}), s32[8,1,2]{2,1,0:T(1,128)S(1)}, u32[]{:S(2)}, u32[]{:S(2)}) %all-to-all-start) | async-done | bytes 96 | tf_op jit(solution)/shard_map/all_to_all | solution.py:42
  24.8 3.5 all-to-all-start.1
  30.4 11.1 %all-to-all-done.1 = bf16[8,2,128,128]{3,2,1,0:T(8,128)(2,1)S(1)} async-done(((bf16[8,2,128,128]{3,2,1,0:T(8,128)(2,1)}), bf16[8,2,128,128]{3,2,1,0:T(8,128)(2,1)S(1)}, u32[]{:S(2)}, u32[]{:S(2)}) %all-to-all-start.1) | async-done | bytes 524320 | tf_op jit(solution)/shard_map/all_to_all | solution.py:50
  41.5 5.5 %fusion.7 = bf16[40,8,128,128]{3,1,2,0:T(8,128)(2,1)} fusion(bf16[2,8,128,128]{3,2,1,0:T(8,128)(2,1)S(1)} %bitcast.92, s32[320]{0:T(512)S(1)} %reduce.1), kind=kOutput, calls=%fused_computation.14 | convolution fusion | flops 173020160 | bytes 11011328 | tf_op jit(solution)/shard_map/dot_general | solution.py:16
  47.0 11.2 %copy.40 = bf16[40,8,128,128]{3,2,1,0:T(8,128)(2,1)} copy(bf16[40,8,128,128]{3,1,2,0:T(8,128)(2,1)} %fusion.7) | data formatting | bytes 20971520
  58.2 13.4 %fusion.6 = f32[320,128,128]{2,1,0:T(8,128)} fusion(bf16[320,128,128]{2,1,0:T(8,128)(2,1)} %bitcast.90, bf16[1,1,320,128,128]{4,3,2,1,0:T(8,128)(2,1)} %param.14, bf16[320]{0:T(512)(128)(2,1)S(1)} %fusion.45), kind=kOutput, calls=%fused_computation.13 | convolution fusion | flops 1347420160 | bytes 41943680 | tf_op jit(solution)/shard_map/kij,kjd->kid/dot_general | solution.py:53
  71.6 25.6 %fusion = f32[32,16384]{1,0:T(8,128)S(1)} fusion(f32[40,8,128,128]{3,2,1,0:T(8,128)} %bitcast.88, s32[320]{0:T(512)S(1)} %reduce), kind=kOutput, calls=%fused_computation.3 | convolution fusion | flops 2013276160 | bytes 23069952 | tf_op jit(solution)/shard_map/dot_general | solution.py:23
  97.3 1.5 reshape_reshape.21
  100.2 9.4 %convert_reduce_fusion = f32[320,128]{1,0:T(8,128)S(1)} fusion(bf16[1,1,320,128,128]{4,3,2,1,0:T(8,128)(2,1)} %param.14, bf16[320]{0:T(512)(128)(2,1)S(1)} %fusion.45), kind=kLoop, calls=%fused_computation.9 | loop fusion | flops 15687680 | bytes 10650240 | tf_op jit(solution)/shard_map/reduce_sum | solution.py:56
  109.8 10.9 %all-reduce = f32[4096]{0:T(1024)S(1)} all-reduce(f32[4096]{0:T(1024)S(1)} %convolution_bitcast_fusion.1), channel_id=3, replica_groups=mesh['row'=8,'col'=4] {'col'}, use_global_device_ids=true, to_apply=%region_2.0.clone | all-reduce | flops 4096 | bytes 32768
  121.0 8.4 %reduce-scatter.2.cloned.1.call-done = f32[1024,128]{1,0:T(8,128)} async-done(((f32[4096,128]{1,0:T(8,128)}), f32[1024,128]{1,0:T(8,128)}) %reduce-scatter.2.cloned.1.call-update) | async-done | bytes 524304 | tf_op jit(solution)/shard_map/reduce_scatter | solution.py:61
  129.4 1.2 divide_convert_fusion
  130.7 1.9 convert_reduce_fusion.1
  132.6 1.0 fusion.14
  133.6 16.8 %all-gather.2.cloned.1.call-done = bf16[4096,128]{1,0:T(8,128)(2,1)} async-done(((bf16[1024,128]{1,0:T(8,128)(2,1)}), bf16[4096,128]{1,0:T(8,128)(2,1)}) %all-gather.2.cloned.1.call-update) | async-done | bytes 1048592 | tf_op jit(solution)/shard_map/all_gather | solution.py:86
  150.4 1.5 reshape_reshape.22
  151.9 5.5 %fusion.8 = bf16[40,8,128,128]{3,1,2,0:T(8,128)(2,1)} fusion(bf16[32,16384]{1,0:T(8,128)(2,1)S(1)} %reshape_reshape.22, s32[320]{0:T(512)S(1)} %reduce), kind=kOutput, calls=%fused_computation.15 | convolution fusion | flops 340797440 | bytes 11535616 | tf_op jit(solution)/shard_map/dot_general | solution.py:16
  157.4 11.2 %copy.42 = bf16[40,8,128,128]{3,2,1,0:T(8,128)(2,1)} copy(bf16[40,8,128,128]{3,1,2,0:T(8,128)(2,1)} %fusion.8) | data formatting | bytes 20971520
  168.6 13.4 %fusion.5 = f32[320,128,128]{2,1,0:T(8,128)} fusion(bf16[320,128,128]{2,1,0:T(8,128)(2,1)} %bitcast.89, bf16[1,1,320,128,128]{4,3,2,1,0:T(8,128)(2,1)} %param.14, bf16[320]{0:T(512)(128)(2,1)S(1)} %fusion.45), kind=kOutput, calls=%fused_computation.12 | convolution fusion | flops 1347420160 | bytes 41943680 | tf_op jit(solution)/shard_map/kij,kid->kjd/dot_general | solution.py:90
  182.1 24.8 %fusion.3 = f32[8,2,128,128]{3,0,2,1:T(8,128)S(1)} fusion(s32[320]{0:T(512)S(1)} %reduce.1, s32[8,2]{0,1:T(2,128)S(1)} %multiply_add_fusion, f32[40,8,128,128]{3,2,1,0:T(8,128)} %bitcast.87), kind=kOutput, calls=%fused_computation.7 | convolution fusion | flops 1006638080 | bytes 22021440 | tf_op jit(solution)/shard_map/dot_general | solution.py:23
  206.9 1.2 copy.30
  208.1 5.5 %all-to-all-start.2 = ((f32[8,2,128,128]{3,2,1,0:T(8,128)}), f32[8,2,128,128]{3,2,1,0:T(8,128)S(1)}, u32[]{:S(2)}, u32[]{:S(2)}) async-start(f32[8,2,128,128]{3,2,1,0:T(8,128)} %copy.30), calls=%async_computation.3 | async-start | bytes 2097152 | tf_op jit(solution)/shard_map/all_to_all | solution.py:93
  213.6 1.0 fusion.47
  214.6 1.0 convolution_bitcast_fusion
  215.6 44.1 %psum.23 = f32[256]{0:T(256)S(1)} all-reduce(f32[256]{0:T(256)S(1)} %get-tuple-element.22), channel_id=1, replica_groups=mesh['row'=8,'col'=4] {'row','col'}, use_global_device_ids=true, to_apply=%region_6.0 | all-reduce | flops 256 | bytes 2048 | tf_op jit(solution)/shard_map/psum | solution.py:77
  260.3 91.4 %all-reduce.4.cloned.1.call-done = (f32[128,256]{0,1:T(8,128)}, f32[128,256]{0,1:T(8,128)}) async-done(((f32[128,256]{0,1:T(8,128)}, f32[128,256]{0,1:T(8,128)}), (f32[128,256]{0,1:T(8,128)}, f32[128,256]{0,1:T(8,128)})) %all-reduce.4.cloned.1.call-update) | async-done | bytes 262160 | tf_op jit(solution)/shard_map/psum | solution.py:77
  351.8 1.0 broadcast_multiply_fusion
  354.3 1.1 fusion.26
  355.4 1.0 fusion.15
  (38 shorter events, 7.3 us)
Async XLA Ops:
  7.2 123.5 %copy-start = (bf16[128,256]{1,0:T(8,128)(2,1)S(1)}, bf16[128,256]{1,0:T(8,128)(2,1)}, u32[]{:S(2)}) copy-start(bf16[128,256]{1,0:T(8,128)(2,1)} %param.12) | copy-start | bytes 196612
  8.6 13.7 %all-to-all-start = ((s32[8,1,2]{2,1,0:T(1,128)}), s32[8,1,2]{2,1,0:T(1,128)S(1)}, u32[]{:S(2)}, u32[]{:S(2)}) async-start(s32[8,1,2]{2,1,0:T(1,128)} %copy.27), calls=%async_computation | async-start | bytes 8192 | tf_op jit(solution)/shard_map/all_to_all | solution.py:42
  24.8 16.8 %all-to-all-start.1 = ((bf16[8,2,128,128]{3,2,1,0:T(8,128)(2,1)}), bf16[8,2,128,128]{3,2,1,0:T(8,128)(2,1)S(1)}, u32[]{:S(2)}, u32[]{:S(2)}) async-start(bf16[8,2,128,128]{3,2,1,0:T(8,128)(2,1)} %bitcast.20), calls=%async_computation.1 | async-start | bytes 1048576 | tf_op jit(solution)/shard_map/all_to_all | solution.py:50
  28.3 101.1 %reduce-scatter.2.cloned.1.call-start = ((), (), s32[]{:S(2)}) async-start(), calls=%async_computation.4 | async-start | bytes 2621440 | tf_op jit(solution)/shard_map/reduce_scatter | solution.py:61
  71.6 27.3 %copy-start.6 = (u32[32]{0:T(128)S(1)}, u32[32]{0:T(128)}, u32[]{:S(2)}) copy-start(u32[32]{0:T(128)} %constant.29) | copy-start | bytes 388
  97.3 23.4 %copy-start.2 = (bf16[1,1024,128]{2,1,0:T(8,128)(2,1)S(1)}, bf16[1,1024,128]{2,1,0:T(8,128)(2,1)}, u32[]{:S(2)}) copy-start(bf16[1,1024,128]{2,1,0:T(8,128)(2,1)} %param.10) | copy-start | bytes 786436
  97.3 23.4 %copy-start.3 = (bf16[128,256]{1,0:T(8,128)(2,1)S(1)}, bf16[128,256]{1,0:T(8,128)(2,1)}, u32[]{:S(2)}) copy-start(bf16[128,256]{1,0:T(8,128)(2,1)} %param.11) | copy-start | bytes 196612
  97.3 33.4 %copy-start.4 = (bf16[1,1024,256]{2,1,0:T(8,128)(2,1)S(1)}, bf16[1,1024,256]{2,1,0:T(8,128)(2,1)}, u32[]{:S(2)}) copy-start(bf16[1,1024,256]{2,1,0:T(8,128)(2,1)} %param.19) | copy-start | bytes 1572868
  97.3 33.4 %copy-start.5 = (f32[256]{0:T(256)S(1)}, f32[256]{0:T(256)}, u32[]{:S(2)}) copy-start(f32[256]{0:T(256)} %param.13) | copy-start | bytes 3076
  98.9 51.5 %all-gather.2.cloned.1.call-start = ((), (), s32[]{:S(2)}) async-start(), calls=%async_computation.5 | async-start | bytes 1310720 | tf_op jit(solution)/shard_map/all_gather | solution.py:86
  182.0 174.4 %copy-start.1 = (bf16[128,256]{1,0:T(8,128)(2,1)S(1)}, bf16[128,256]{1,0:T(8,128)(2,1)}, u32[]{:S(2)}) copy-start(bf16[128,256]{1,0:T(8,128)(2,1)} %param.12) | copy-start | bytes 196612
  208.1 146.2 %all-to-all-start.2 = ((f32[8,2,128,128]{3,2,1,0:T(8,128)}), f32[8,2,128,128]{3,2,1,0:T(8,128)S(1)}, u32[]{:S(2)}, u32[]{:S(2)}) async-start(f32[8,2,128,128]{3,2,1,0:T(8,128)} %copy.30), calls=%async_computation.3 | async-start | bytes 2097152 | tf_op jit(solution)/shard_map/all_to_all | solution.py:93
  213.6 138.2 %all-reduce.4.cloned.1.call-start = ((), (), s32[]{:S(2)}) async-start(), calls=%async_computation.6 | async-start | bytes 524288 | tf_op jit(solution)/shard_map/psum | solution.py:77
Sparse Core Ops, SparseCore 0:
  99.0 30.3 reduce-scatter.1
  133.7 16.6 all-gather.1
  220.6 131.1 all-reduce.3
where the time goes:
time: 369 us; the launch traced here: 363 us
  waiting for transfers between devices  133 us (36%)
  matrix products  96 us (26%)
  blocking collectives  55.1 us (15%)
  local copies, waits for them, and re-layouts  32.8 us (9%)
  starting transfers between devices  16.4 us (4%)
  between operations  15.7 us (4%)
  other arithmetic  14.3 us (4%)
    psum x1, waiting for transfers between devices, on_device(): lax.psum((local_self, local_neigh, local_bias), ('row', 'col'))  91.4 us
    dot_general x4, matrix products, group_rows(): jnp.dot(grouper, flat, precision=lax.Precision.HIGHEST, preferred_element...  51.7 us
    psum x1, blocking collectives, on_device(): lax.psum((local_self, local_neigh, local_bias), ('row', 'col'))  44.1 us
    unnamed x20, local copies, waits for them, and re-layouts  25.4 us
    all_gather x1, waiting for transfers between devices, on_device(): adjoint_panel = lax.all_gather(grad_agg, 'col', axis=0, tiled=True)  16.8 us
    dot_general x1, matrix products, on_device(): jnp.einsum('kij,kid->kjd', adjacency, row_pieces, preferred_element_type=...  13.4 us
    dot_general x1, matrix products, on_device(): jnp.einsum('kij,kjd->kid', adjacency, gathered, preferred_element_type=jn...  13.4 us
    dot_general x3, matrix products, select_rows(): jnp.dot(picker, flat, preferred_element_type=jnp.float32)  11.3 us
  transfers between devices with their start and end apart: 6, of which 5 were waited for; matrix products, arithmetic and copies ran while one was open for 5% of the time, Pallas kernels for 0%

commit v1 on v0

v1 whole, which is shorter than its diff:
```python
import functools
import math

import jax
import jax.numpy as jnp
from jax import lax
from jax.experimental import pallas as pl
from jax.experimental.pallas import tpu as pltpu
from jax.sharding import PartitionSpec as P

GROUP = 32


def gelu_tanh(values):
    return jax.nn.gelu(values, approximate=True)


def select_rows(indices, table, total):
    picker = (indices[:, None] == jnp.arange(total, dtype=jnp.int32)[None, :]).astype(table.dtype)
    flat = table.reshape(total, -1)
    taken = jnp.dot(picker, flat, preferred_element_type=jnp.float32).astype(table.dtype)
    return taken.reshape((indices.shape[0],) + table.shape[1:])


def group_rows(indices, values, total):
    grouper = (jnp.arange(total, dtype=jnp.int32)[:, None] == indices[None, :]).astype(jnp.float32)
    flat = values.reshape(values.shape[0], -1)
    added = jnp.dot(
        grouper, flat, precision=lax.Precision.HIGHEST, preferred_element_type=jnp.float32
    )
    return added.reshape((total,) + values.shape[1:])


def _live_group(g, count_ref):
    return jnp.minimum(g, (count_ref[0] - 1) // GROUP)


def _forward_kernel(count_ref, row_ref, slot_ref, blk_ref, feat_ref, sum_ref, deg_ref):
    g = pl.program_id(0)

    @pl.when(g == 0)
    def _():
        sum_ref[...] = jnp.zeros_like(sum_ref)
        deg_ref[...] = jnp.zeros_like(deg_ref)

    count = count_ref[0]
    ones = jnp.ones((8, blk_ref.shape[-1]), jnp.bfloat16)
    for j in range(GROUP):
        k = g * GROUP + j

        @pl.when(k < count)
        def _():
            blk = blk_ref[j]
            r = row_ref[k]
            s = slot_ref[k]
            sum_ref[r] += jnp.dot(blk, feat_ref[s], preferred_element_type=jnp.float32)
            deg_ref[r] += lax.dot_general(
                ones, blk, (((1,), (1,)), ((), ())), preferred_element_type=jnp.float32
            )


def _backward_kernel(count_ref, row_ref, slot_ref, blk_ref, grad_ref, out_ref):
    g = pl.program_id(0)

    @pl.when(g == 0)
    def _():
        out_ref[...] = jnp.zeros_like(out_ref)

    count = count_ref[0]
    for j in range(GROUP):
        k = g * GROUP + j

        @pl.when(k < count)
        def _():
            blk = blk_ref[j]
            r = row_ref[k]
            s = slot_ref[k]
            out_ref[s] += lax.dot_general(
                blk, grad_ref[r], (((0,), (0,)), ((), ())), preferred_element_type=jnp.float32
            )


def aggregate_forward(counts, rows, slots, blocks, fetched, panel_blocks):
    slot_total, bs, _ = blocks.shape
    fetch_total, _, width = fetched.shape
    grid_spec = pltpu.PrefetchScalarGridSpec(
        num_scalar_prefetch=3,
        grid=(slot_total // GROUP,),
        in_specs=[
            pl.BlockSpec((GROUP, bs, bs), lambda g, c, r, s: (_live_group(g, c), 0, 0)),
            pl.BlockSpec((fetch_total, bs, width), lambda g, c, r, s: (0, 0, 0)),
        ],
        out_specs=[
            pl.BlockSpec((panel_blocks, bs, width), lambda g, c, r, s: (0, 0, 0)),
            pl.BlockSpec((panel_blocks, 8, bs), lambda g, c, r, s: (0, 0, 0)),
        ],
    )
    flops = 2 * slot_total * bs * bs * (width + 8)
    return pl.pallas_call(
        _forward_kernel,
        grid_spec=grid_spec,
        out_shape=[
            jax.ShapeDtypeStruct((panel_blocks, bs, width), jnp.float32),
            jax.ShapeDtypeStruct((panel_blocks, 8, bs), jnp.float32),
        ],
        compiler_params=pltpu.CompilerParams(dimension_semantics=("arbitrary",)),
        cost_estimate=pl.CostEstimate(
            flops=flops,
            bytes_accessed=blocks.size * 2 + fetched.size * 2 + panel_blocks * bs * (width + 8) * 4,
            transcendentals=0,
        ),
    )(counts, rows, slots, blocks, fetched)


def aggregate_backward(counts, rows, slots, blocks, grad_panel, fetch_total):
    slot_total, bs, _ = blocks.shape
    panel_blocks, _, width = grad_panel.shape
    grid_spec = pltpu.PrefetchScalarGridSpec(
        num_scalar_prefetch=3,
        grid=(slot_total // GROUP,),
        in_specs=[
            pl.BlockSpec((GROUP, bs, bs), lambda g, c, r, s: (_live_group(g, c), 0, 0)),
            pl.BlockSpec((panel_blocks, bs, width), lambda g, c, r, s: (0, 0, 0)),
        ],
        out_specs=pl.BlockSpec((fetch_total, bs, width), lambda g, c, r, s: (0, 0, 0)),
    )
    return pl.pallas_call(
        _backward_kernel,
        grid_spec=grid_spec,
        out_shape=jax.ShapeDtypeStruct((fetch_total, bs, width), jnp.float32),
        compiler_params=pltpu.CompilerParams(dimension_semantics=("arbitrary",)),
        cost_estimate=pl.CostEstimate(
            flops=2 * slot_total * bs * bs * width,
            bytes_accessed=blocks.size * 2 + grad_panel.size * 2 + fetch_total * bs * width * 4,
            transcendentals=0,
        ),
    )(counts, rows, slots, blocks, grad_panel)


def all_sum(values, axes):
    for name in axes:
        size = lax.axis_size(name)
        step = 1
        while step < size:
            pairs = [(i, i ^ step) for i in range(size)]
            values = values + lax.ppermute(values, name, pairs)
            step *= 2
    return values


def on_device(
    features, w_self, w_neigh, bias, blocks, blk_row, blk_slot, counts, col_list, cotangent
):
    own_feats = features[0]
    node_count, feat_width = own_feats.shape
    block_size = blocks.shape[-1]
    owned_count = node_count // block_size
    row_count = lax.axis_size("row")
    col_count = lax.axis_size("col")
    picks_each = col_list.shape[-1]
    fetch_total = row_count * picks_each
    panel_blocks = col_count * owned_count
    wanted = col_list[0, 0]
    asked_for = lax.all_to_all(wanted, "row", split_axis=0, concat_axis=0, tiled=True)
    block_rows = blk_row[0, 0]
    block_slots = blk_slot[0, 0]
    live_count = counts[0, 0]
    own_blocks = own_feats.reshape(owned_count, block_size, feat_width)
    outgoing = select_rows(asked_for.reshape(-1), own_blocks, owned_count)
    outgoing = outgoing.reshape(row_count, picks_each, block_size, feat_width)
    arrived = lax.all_to_all(outgoing, "row", split_axis=0, concat_axis=0, tiled=True)
    fetched = arrived.reshape(fetch_total, block_size, feat_width)
    part_sums, part_deg = aggregate_forward(
        live_count, block_rows, block_slots, blocks[0, 0], fetched, panel_blocks
    )
    part_sums = part_sums.reshape(col_count, node_count, feat_width)
    part_deg = part_deg[:, 0, :].reshape(col_count, owned_count, block_size)
    part_deg = jnp.pad(part_deg, ((0, 0), (0, 16 - owned_count), (0, 0)))
    packed = jnp.concatenate([part_sums, part_deg], axis=1)
    packed = packed.reshape(col_count * (node_count + 16), feat_width)
    reduced = lax.psum_scatter(packed, "col", scatter_dimension=0, tiled=True)
    summed = reduced[:node_count]
    degree = reduced[node_count : node_count + owned_count].reshape(node_count)
    divisor = 1.0 + degree
    neighbors = (summed / divisor[:, None]).astype(jnp.bfloat16)
    hidden = (
        jnp.dot(own_feats, w_self, preferred_element_type=jnp.float32)
        + jnp.dot(neighbors, w_neigh, preferred_element_type=jnp.float32)
        + bias
    )
    output, pullback = jax.vjp(gelu_tanh, hidden)
    grad_hidden = pullback(cotangent[0].astype(jnp.float32))[0]
    grad_round = grad_hidden.astype(jnp.bfloat16)
    local_self = jnp.einsum("nd,nh->dh", own_feats, grad_round, preferred_element_type=jnp.float32)
    local_neigh = jnp.einsum("nd,nh->dh", neighbors, grad_round, preferred_element_type=jnp.float32)
    local_bias = jnp.sum(grad_round.astype(jnp.float32), axis=0)
    hid = local_bias.shape[0]
    weight_pack = jnp.concatenate(
        [local_self, local_neigh, jnp.broadcast_to(local_bias[None], (8, hid))], axis=0
    )
    weight_pack = all_sum(weight_pack, ("col", "row"))
    factor = 1.0 / math.sqrt(node_count * row_count * col_count)
    grad_self = weight_pack[:feat_width] * factor
    grad_neigh = weight_pack[feat_width : 2 * feat_width] * factor
    grad_bias = weight_pack[2 * feat_width] * factor
    grad_agg = (
        jnp.einsum("nh,dh->nd", grad_round, w_neigh, preferred_element_type=jnp.float32)
        / divisor[:, None]
    )
    grad_agg = grad_agg.astype(jnp.bfloat16)
    adjoint_panel = lax.all_gather(grad_agg, "col", axis=0, tiled=True)
    per_slot = aggregate_backward(
        live_count,
        block_rows,
        block_slots,
        blocks[0, 0],
        adjoint_panel.reshape(panel_blocks, block_size, feat_width),
        fetch_total,
    )
    per_slot = per_slot.reshape(row_count, picks_each, block_size, feat_width)
    returned = lax.all_to_all(per_slot, "row", split_axis=0, concat_axis=0, tiled=True)
    incoming = group_rows(
        asked_for.reshape(-1),
        returned.reshape(fetch_total, block_size, feat_width),
        owned_count,
    )
    incoming = incoming.reshape(node_count, feat_width)
    grad_feats = (
        jnp.einsum("nh,dh->nd", grad_round, w_self, preferred_element_type=jnp.float32) + incoming
    )
    return (
        output.astype(jnp.bfloat16)[None],
        grad_feats.astype(jnp.bfloat16)[None],
        grad_self,
        grad_neigh,
        grad_bias,
    )


def solution(mesh):
    return jax.shard_map(
        on_device,
        mesh=mesh,
        in_specs=(
            P("col", "row", None),
            P(),
            P(),
            P(),
            P("row", "col", None, None, None),
            P("row", "col", None),
            P("row", "col", None),
            P("row", "col", None),
            P("row", "col", None, None),
            P("col", "row", None),
        ),
        out_specs=(P("col", "row", None), P("col", "row", None), P(), P(), P()),
        check_vma=False,
    )
```

time: 369 us -> 270 us (0.73)
  Pallas kernels: 0 us -> 115 us
  matrix products: 96 us -> 6.11 us
  blocking collectives: 55.1 us -> 0 us
  waiting for transfers between devices: 133 us -> 97.5 us
  local copies, waits for them, and re-layouts: 32.8 us -> 5.75 us
  other arithmetic: 14.3 us -> 8.38 us
  starting transfers between devices: 16.4 us -> 20.3 us
    pallas_call x0 -> x2, Pallas kernels: none -> 115 us  [the longest x1 62.9 us: aggregate_backward(): pl.pallas_call(_backward_kernel, grid_spec=grid_spec, out_shape=jax.Shape...]
    psum x1 -> x0, waiting for transfers between devices: 91.4 us -> none  [on_device(): lax.psum((local_self, local_neigh, local_bias), ('row', 'col'))]
    dot_general x4 -> x1, matrix products: 51.7 us -> 1.05 us  [group_rows(): jnp.dot(grouper, flat, precision=lax.Precision.HIGHEST, preferred_element...]
    psum x1 -> x0, blocking collectives: 44.1 us -> none  [on_device(): lax.psum((local_self, local_neigh, local_bias), ('row', 'col'))]
    ppermute x0 -> x5, waiting for transfers between devices: none -> 36.7 us  [all_sum(): values = values + lax.ppermute(values, name, pairs)]
    dot_general x2 -> x0, matrix products: 26.8 us -> none  [the longest x1 13.4 us: on_device(): jnp.einsum('kij,kid->kjd', adjacency, row_pieces, preferred_element_type=...]
    unnamed x20 -> x17, local copies, waits for them, and re-layouts: 25.4 us -> 1.72 us
    reduce_scatter x1, waiting for transfers between devices: 8.39 us -> 27.9 us  [on_device(): reduced = lax.psum_scatter(packed, 'col', scatter_dimension=0, tiled=True)]
  transfers between devices with their start and end apart: 6 -> 10, of which waited for: 5 -> 8; matrix products, arithmetic and copies ran while one was open for 5% -> 2% of each run, Pallas kernels for 0% -> 23%
where the time goes in v1:
time: 270 us; the launch traced here: 268 us
  Pallas kernels  115 us (43%)
  waiting for transfers between devices  97.5 us (36%)
  starting transfers between devices  20.3 us (8%)
  between operations  14.9 us (6%)
  other arithmetic  8.38 us (3%)
  matrix products  6.11 us (2%)
  local copies, waits for them, and re-layouts  5.75 us (2%)
    pallas_call x1, Pallas kernels, aggregate_backward(): pl.pallas_call(_backward_kernel, grid_spec=grid_spec, out_shape=jax.Shape...  62.9 us
    pallas_call x1, Pallas kernels, aggregate_forward(): pl.pallas_call(_forward_kernel, grid_spec=grid_spec, out_shape=[jax.Shape...  52 us
    ppermute x5, waiting for transfers between devices, all_sum(): values = values + lax.ppermute(values, name, pairs)  36.7 us
    reduce_scatter x1, waiting for transfers between devices, on_device(): reduced = lax.psum_scatter(packed, 'col', scatter_dimension=0, tiled=True)  27.9 us
    all_gather x1, waiting for transfers between devices, on_device(): adjoint_panel = lax.all_gather(grad_agg, 'col', axis=0, tiled=True)  16.2 us
    all_to_all x1, waiting for transfers between devices, on_device(): lax.all_to_all(outgoing, 'row', split_axis=0, concat_axis=0, tiled=True)  11.3 us
    all_to_all x1, starting transfers between devices, on_device(): lax.all_to_all(wanted, 'row', split_axis=0, concat_axis=0, tiled=True)  7.31 us
  transfers between devices with their start and end apart: 10, of which 8 were waited for; matrix products, arithmetic and copies ran while one was open for 2% of the time, Pallas kernels for 23%

profile of v1, /device:TPU:0, one launch (start us, length us, event | category | flops | bytes accessed | tf_op | source)
XLA Modules:
  0.0 267.9 jit_solution(12924647966050519628)
XLA Ops:
  7.2 1.4 copy.17
  8.6 7.3 %all-to-all-start = ((s32[8,1,2]{2,1,0:T(1,128)}), s32[8,1,2]{2,1,0:T(1,128)S(1)}, u32[]{:S(2)}, u32[]{:S(2)}) async-start(s32[8,1,2]{2,1,0:T(1,128)} %copy.17), calls=%async_computation | async-start | bytes 8192 | tf_op jit(solution)/shard_map/all_to_all | solution.py:164
  15.9 1.1 reshape_reshape_squeeze.3
  17.0 5.4 %all-to-all-done = s32[8,1,2]{2,1,0:T(1,128)S(1)} async-done(((s32[8,1,2]{2,1,0:T(1,128)}), s32[8,1,2]{2,1,0:T(1,128)S(1)}, u32[]{:S(2)}, u32[]{:S(2)}) %all-to-all-start) | async-done | bytes 96 | tf_op jit(solution)/shard_map/all_to_all | solution.py:164
  22.8 0.7 reduce.5
  23.9 0.9 copy.18
  24.8 3.5 %all-to-all-start.1 = ((bf16[8,2,128,128]{3,2,1,0:T(8,128)(2,1)}), bf16[8,2,128,128]{3,2,1,0:T(8,128)(2,1)S(1)}, u32[]{:S(2)}, u32[]{:S(2)}) async-start(bf16[8,2,128,128]{3,2,1,0:T(8,128)(2,1)} %bitcast.19), calls=%async_computation.1 | async-start | bytes 1048576 | tf_op jit(solution)/shard_map/all_to_all | solution.py:171
  28.4 0.6 reduce.row_ref
  29.0 0.6 reduce.1.slot_ref
  30.2 11.3 %all-to-all-done.1 = bf16[8,2,128,128]{3,2,1,0:T(8,128)(2,1)S(1)} async-done(((bf16[8,2,128,128]{3,2,1,0:T(8,128)(2,1)}), bf16[8,2,128,128]{3,2,1,0:T(8,128)(2,1)S(1)}, u32[]{:S(2)}, u32[]{:S(2)}) %all-to-all-start.1) | async-done | bytes 524320 | tf_op jit(solution)/shard_map/all_to_all | solution.py:171
  41.6 0.8 copy-done.2
  42.4 52.0 %shard_map.137 = (f32[32,128,128]{2,1,0:T(8,128)}, f32[32,8,128]{2,1,0:T(8,128)}) custom-call(s32[1]{0:T(128)} %bitcast.47.count_ref, s32[320]{0:T(512)} %reduce.row_ref, s32[320]{0:T(512)} %reduce.1.slot_ref, bf16[320,128,128]{2,1,0:T(8,128)(2,1)} %bitcast.49, bf16[16,128,128]{2,1,0:T(8,128)(2,1)} %bitcast.54), custom_call_target="tpu_custom_call" | custom-call | flops 1426063360 | bytes 13238272 | tf_op jit(solution)/shard_map/pallas_call | solution.py:99
  94.4 0.9 slice.18
  95.3 3.1 %select_maximum_fusion = f32[4,1040,128]{2,1,0:T(8,128)} fusion(f32[4,8,128]{2,1,0:T(8,128)S(1)} %bitcast.57, f32[4,1024,128]{2,1,0:T(8,128)} %bitcast.55), kind=kLoop, calls=%fused_computation.1 | loop fusion | flops 1597440 | bytes 4243456 | tf_op jit(solution)/shard_map/concatenate | solution.py:179
  98.8 27.9 %reduce-scatter.2.cloned.1.call-done = f32[1040,128]{1,0:T(8,128)} async-done(((f32[4160,128]{1,0:T(8,128)}), f32[1040,128]{1,0:T(8,128)}) %reduce-scatter.2.cloned.1.call-update) | async-done | bytes 532496 | tf_op jit(solution)/shard_map/reduce_scatter | solution.py:181
  126.7 0.7 fusion.23
  127.4 1.2 fusion.18
  128.7 1.9 convert_reduce_fusion
  130.5 1.0 fusion.3
  132.2 16.2 %all-gather.2.cloned.1.call-done = bf16[4096,128]{1,0:T(8,128)(2,1)} async-done(((bf16[1024,128]{1,0:T(8,128)(2,1)}), bf16[4096,128]{1,0:T(8,128)(2,1)}) %all-gather.2.cloned.1.call-update) | async-done | bytes 1048592 | tf_op jit(solution)/shard_map/all_gather | solution.py:211
  148.4 62.9 %shard_map.138 = f32[16,128,128]{2,1,0:T(8,128)} custom-call(s32[1]{0:T(128)} %bitcast.48.count_ref, s32[320]{0:T(512)} %reduce.row_ref, s32[320]{0:T(512)} %reduce.1.slot_ref, bf16[320,128,128]{2,1,0:T(8,128)(2,1)} %bitcast.50, bf16[32,128,128]{2,1,0:T(8,128)(2,1)} %bitcast.56), custom_call_target="tpu_custom_call" | custom-call | flops 1342177280 | bytes 12582912 | tf_op jit(solution)/shard_map/pallas_call | solution.py:127
  211.3 4.2 %all-to-all-start.2 = ((f32[8,2,128,128]{3,2,1,0:T(8,128)}), f32[8,2,128,128]{3,2,1,0:T(8,128)S(1)}, u32[]{:S(2)}, u32[]{:S(2)}) async-start(f32[8,2,128,128]{3,2,1,0:T(8,128)} %bitcast.52), calls=%async_computation.3 | async-start | bytes 2097152 | tf_op jit(solution)/shard_map/all_to_all | solution.py:221
  215.7 7.0 %collective-permute-done.1 = f32[264,256]{1,0:T(8,128)S(1)} collective-permute-done((f32[264,256]{1,0:T(8,128)S(1)}, f32[264,256]{1,0:T(8,128)S(1)}, u32[]{:S(2)}, u32[]{:S(2)}) %collective-permute-start.1) | collective-permute-done | bytes 270368 | tf_op jit(solution)/shard_map/ppermute | solution.py:146
  222.8 1.7 collective-permute-start.2
  224.4 8.6 %collective-permute-done.2 = f32[264,256]{1,0:T(8,128)S(1)} collective-permute-done((f32[264,256]{1,0:T(8,128)S(1)}, f32[264,256]{1,0:T(8,128)S(1)}, u32[]{:S(2)}, u32[]{:S(2)}) %collective-permute-start.2) | collective-permute-done | bytes 270368 | tf_op jit(solution)/shard_map/ppermute | solution.py:146
  233.1 1.6 collective-permute-start.3
  234.7 9.0 %collective-permute-done.3 = f32[264,256]{1,0:T(8,128)S(1)} collective-permute-done((f32[264,256]{1,0:T(8,128)S(1)}, f32[264,256]{1,0:T(8,128)S(1)}, u32[]{:S(2)}, u32[]{:S(2)}) %collective-permute-start.3) | collective-permute-done | bytes 270368 | tf_op jit(solution)/shard_map/ppermute | solution.py:146
  243.8 1.7 collective-permute-start.4
  245.5 12.0 %collective-permute-done.4 = f32[264,256]{1,0:T(8,128)S(1)} collective-permute-done((f32[264,256]{1,0:T(8,128)S(1)}, f32[264,256]{1,0:T(8,128)S(1)}, u32[]{:S(2)}, u32[]{:S(2)}) %collective-permute-start.4) | collective-permute-done | bytes 270368 | tf_op jit(solution)/shard_map/ppermute | solution.py:146
  258.1 0.7 slice_multiply_fusion
  258.9 1.1 fusion.15
  260.0 1.0 fusion.4
  (38 shorter events, 2.9 us)
Async XLA Ops:
  7.2 121.5 %copy-start = (bf16[128,256]{1,0:T(8,128)(2,1)S(1)}, bf16[128,256]{1,0:T(8,128)(2,1)}, u32[]{:S(2)}) copy-start(bf16[128,256]{1,0:T(8,128)(2,1)} %param.12) | copy-start | bytes 196612
  7.2 21.2 %copy-start.4 = (s32[1,1,320]{2,1,0:T(1,128)S(1)}, s32[1,1,320]{2,1,0:T(1,128)}, u32[]{:S(2)}) copy-start(s32[1,1,320]{2,1,0:T(1,128)} %param.15) | copy-start | bytes 3844
  7.2 21.8 %copy-start.5 = (s32[1,1,320]{2,1,0:T(1,128)S(1)}, s32[1,1,320]{2,1,0:T(1,128)}, u32[]{:S(2)}) copy-start(s32[1,1,320]{2,1,0:T(1,128)} %param.16) | copy-start | bytes 3844
  8.6 13.7 %all-to-all-start = ((s32[8,1,2]{2,1,0:T(1,128)}), s32[8,1,2]{2,1,0:T(1,128)S(1)}, u32[]{:S(2)}, u32[]{:S(2)}) async-start(s32[8,1,2]{2,1,0:T(1,128)} %copy.17), calls=%async_computation | async-start | bytes 8192 | tf_op jit(solution)/shard_map/all_to_all | solution.py:164
  24.8 16.8 %all-to-all-start.1 = ((bf16[8,2,128,128]{3,2,1,0:T(8,128)(2,1)}), bf16[8,2,128,128]{3,2,1,0:T(8,128)(2,1)S(1)}, u32[]{:S(2)}, u32[]{:S(2)}) async-start(bf16[8,2,128,128]{3,2,1,0:T(8,128)(2,1)} %bitcast.19), calls=%async_computation.1 | async-start | bytes 1048576 | tf_op jit(solution)/shard_map/all_to_all | solution.py:171
  28.3 98.4 %reduce-scatter.2.cloned.1.call-start = ((), (), s32[]{:S(2)}) async-start(), calls=%async_computation.4 | async-start | bytes 2662400 | tf_op jit(solution)/shard_map/reduce_scatter | solution.py:181
  41.6 0.8 copy-start.2
  95.3 3.2 %copy-start.1 = (bf16[1,1024,128]{2,1,0:T(8,128)(2,1)S(1)}, bf16[1,1024,128]{2,1,0:T(8,128)(2,1)}, u32[]{:S(2)}) copy-start(bf16[1,1024,128]{2,1,0:T(8,128)(2,1)} %param.10) | copy-start | bytes 786436
  95.3 3.2 %copy-start.3 = (bf16[128,256]{1,0:T(8,128)(2,1)S(1)}, bf16[128,256]{1,0:T(8,128)(2,1)}, u32[]{:S(2)}) copy-start(bf16[128,256]{1,0:T(8,128)(2,1)} %param.11) | copy-start | bytes 196612
  98.5 30.2 %copy-start.6 = (bf16[1,1024,256]{2,1,0:T(8,128)(2,1)S(1)}, bf16[1,1024,256]{2,1,0:T(8,128)(2,1)}, u32[]{:S(2)}) copy-start(bf16[1,1024,256]{2,1,0:T(8,128)(2,1)} %param.19) | copy-start | bytes 1572868
  98.5 30.2 %copy-start.7 = (f32[256]{0:T(256)S(1)}, f32[256]{0:T(256)}, u32[]{:S(2)}) copy-start(f32[256]{0:T(256)} %param.13) | copy-start | bytes 3076
  98.5 49.9 %all-gather.2.cloned.1.call-start = ((), (), s32[]{:S(2)}) async-start(), calls=%async_computation.5 | async-start | bytes 1310720 | tf_op jit(solution)/shard_map/all_gather | solution.py:211
  132.2 83.4 %collective-permute-start = (f32[264,256]{1,0:T(8,128)S(1)}, f32[264,256]{1,0:T(8,128)S(1)}, u32[]{:S(2)}, u32[]{:S(2)}) collective-permute-start(f32[264,256]{1,0:T(8,128)S(1)} %pad_maximum_fusion), channel_id=1, source_target_pairs={{0,1},{1,0},{2,3},{3,2},{4,5},{5,4},{6,7},{7,6},{8,9},{9,8},{10,11... | collective-permute-start | bytes 811016 | tf_op jit(solution)/shard_map/ppermute | solution.py:146
  211.3 47.5 %all-to-all-start.2 = ((f32[8,2,128,128]{3,2,1,0:T(8,128)}), f32[8,2,128,128]{3,2,1,0:T(8,128)S(1)}, u32[]{:S(2)}, u32[]{:S(2)}) async-start(f32[8,2,128,128]{3,2,1,0:T(8,128)} %bitcast.52), calls=%async_computation.3 | async-start | bytes 2097152 | tf_op jit(solution)/shard_map/all_to_all | solution.py:221
  215.6 7.1 %collective-permute-start.1 = (f32[264,256]{1,0:T(8,128)S(1)}, f32[264,256]{1,0:T(8,128)S(1)}, u32[]{:S(2)}, u32[]{:S(2)}) collective-permute-start(f32[264,256]{1,0:T(8,128)S(1)} %fusion.26), channel_id=1, source_target_pairs={{0,2},{1,3},{2,0},{3,1},{4,6},{5,7},{6,4},{7,5},{8,10},{9,11},{10,... | collective-permute-start | bytes 811016 | tf_op jit(solution)/shard_map/ppermute | solution.py:146
  222.8 10.3 %collective-permute-start.2 = (f32[264,256]{1,0:T(8,128)S(1)}, f32[264,256]{1,0:T(8,128)S(1)}, u32[]{:S(2)}, u32[]{:S(2)}) collective-permute-start(f32[264,256]{1,0:T(8,128)S(1)} %add.63), channel_id=1, source_target_pairs={{0,4},{4,0},{8,12},{12,8},{16,20},{20,16},{24,28},{28,24},{1,5},{5... | collective-permute-start | bytes 811016 | tf_op jit(solution)/shard_map/ppermute | solution.py:146
  233.1 10.6 %collective-permute-start.3 = (f32[264,256]{1,0:T(8,128)S(1)}, f32[264,256]{1,0:T(8,128)S(1)}, u32[]{:S(2)}, u32[]{:S(2)}) collective-permute-start(f32[264,256]{1,0:T(8,128)S(1)} %add.64), channel_id=1, source_target_pairs={{0,8},{4,12},{8,0},{12,4},{16,24},{20,28},{24,16},{28,20},{1,9},{5... | collective-permute-start | bytes 811016 | tf_op jit(solution)/shard_map/ppermute | solution.py:146
  243.8 13.8 %collective-permute-start.4 = (f32[264,256]{1,0:T(8,128)S(1)}, f32[264,256]{1,0:T(8,128)S(1)}, u32[]{:S(2)}, u32[]{:S(2)}) collective-permute-start(f32[264,256]{1,0:T(8,128)S(1)} %add.65), channel_id=1, source_target_pairs={{0,16},{4,20},{8,24},{12,28},{16,0},{20,4},{24,8},{28,12},{1,17},{... | collective-permute-start | bytes 811016 | tf_op jit(solution)/shard_map/ppermute | solution.py:146
Sparse Core Ops, SparseCore 0:
  98.6 28.0 reduce-scatter.1
  131.7 16.6 all-gather.1

commit v2 on v1

--- a/solution.py
+++ b/solution.py
@@ -45,18 +45,21 @@
 
     count = count_ref[0]
     ones = jnp.ones((8, blk_ref.shape[-1]), jnp.bfloat16)
-    for j in range(GROUP):
-        k = g * GROUP + j
-
-        @pl.when(k < count)
-        def _():
+
+    @pl.when(g * GROUP < count)
+    def _():
+        for j in range(GROUP):
+            k = g * GROUP + j
+            live = k < count
             blk = blk_ref[j]
             r = row_ref[k]
             s = slot_ref[k]
-            sum_ref[r] += jnp.dot(blk, feat_ref[s], preferred_element_type=jnp.float32)
-            deg_ref[r] += lax.dot_general(
+            prod = jnp.dot(blk, feat_ref[s], preferred_element_type=jnp.float32)
+            rsum = lax.dot_general(
                 ones, blk, (((1,), (1,)), ((), ())), preferred_element_type=jnp.float32
             )
+            sum_ref[r] += jnp.where(live, prod, 0.0)
+            deg_ref[r] += jnp.where(live, rsum, 0.0)
 
 
 def _backward_kernel(count_ref, row_ref, slot_ref, blk_ref, grad_ref, out_ref):
@@ -67,17 +70,17 @@
         out_ref[...] = jnp.zeros_like(out_ref)
 
     count = count_ref[0]
-    for j in range(GROUP):
-        k = g * GROUP + j
-
-        @pl.when(k < count)
-        def _():
+
+    @pl.when(g * GROUP < count)
+    def _():
+        for j in range(GROUP):
+            k = g * GROUP + j
+            live = k < count
             blk = blk_ref[j]
             r = row_ref[k]
             s = slot_ref[k]
-            out_ref[s] += lax.dot_general(
-                blk, grad_ref[r], (((0,), (0,)), ((), ())), preferred_element_type=jnp.float32
-            )
+            prod = jnp.dot(grad_ref[r], blk, preferred_element_type=jnp.float32)
+            out_ref[s] += jnp.where(live, prod, 0.0)
 
 
 def aggregate_forward(counts, rows, slots, blocks, fetched, panel_blocks):
@@ -114,20 +117,20 @@
 
 def aggregate_backward(counts, rows, slots, blocks, grad_panel, fetch_total):
     slot_total, bs, _ = blocks.shape
-    panel_blocks, _, width = grad_panel.shape
+    panel_blocks, width, _ = grad_panel.shape
     grid_spec = pltpu.PrefetchScalarGridSpec(
         num_scalar_prefetch=3,
         grid=(slot_total // GROUP,),
         in_specs=[
             pl.BlockSpec((GROUP, bs, bs), lambda g, c, r, s: (_live_group(g, c), 0, 0)),
-            pl.BlockSpec((panel_blocks, bs, width), lambda g, c, r, s: (0, 0, 0)),
-        ],
-        out_specs=pl.BlockSpec((fetch_total, bs, width), lambda g, c, r, s: (0, 0, 0)),
+            pl.BlockSpec((panel_blocks, width, bs), lambda g, c, r, s: (0, 0, 0)),
+        ],
+        out_specs=pl.BlockSpec((fetch_total, width, bs), lambda g, c, r, s: (0, 0, 0)),
     )
     return pl.pallas_call(
         _backward_kernel,
         grid_spec=grid_spec,
-        out_shape=jax.ShapeDtypeStruct((fetch_total, bs, width), jnp.float32),
+        out_shape=jax.ShapeDtypeStruct((fetch_total, width, bs), jnp.float32),
         compiler_params=pltpu.CompilerParams(dimension_semantics=("arbitrary",)),
         cost_estimate=pl.CostEstimate(
             flops=2 * slot_total * bs * bs * width,
@@ -209,15 +212,11 @@
     )
     grad_agg = grad_agg.astype(jnp.bfloat16)
     adjoint_panel = lax.all_gather(grad_agg, "col", axis=0, tiled=True)
-    per_slot = aggregate_backward(
-        live_count,
-        block_rows,
-        block_slots,
-        blocks[0, 0],
-        adjoint_panel.reshape(panel_blocks, block_size, feat_width),
-        fetch_total,
-    )
-    per_slot = per_slot.reshape(row_count, picks_each, block_size, feat_width)
+    panel_t = adjoint_panel.reshape(panel_blocks, block_size, feat_width).transpose(0, 2, 1)
+    per_slot_t = aggregate_backward(
+        live_count, block_rows, block_slots, blocks[0, 0], panel_t, fetch_total
+    )
+    per_slot = per_slot_t.transpose(0, 2, 1).reshape(row_count, picks_each, block_size, feat_width)
     returned = lax.all_to_all(per_slot, "row", split_axis=0, concat_axis=0, tiled=True)
     incoming = group_rows(
         asked_for.reshape(-1),

time: 270 us -> 191 us (0.71); the launches traced: 268 us -> 192 us
  Pallas kernels: 115 us -> 26.9 us
  waiting for transfers between devices: 97.5 us -> 104 us
  local copies, waits for them, and re-layouts: 5.75 us -> 10.5 us
    pallas_call x1, Pallas kernels: 62.9 us -> 11.4 us  [aggregate_backward(): pl.pallas_call(_backward_kernel, grid_spec=grid_spec, out_shape=jax.Shape...]
    pallas_call x1, Pallas kernels: 52 us -> 15.4 us  [aggregate_forward(): pl.pallas_call(_forward_kernel, grid_spec=grid_spec, out_shape=[jax.Shape...]
    reshape x0 -> x2, local copies, waits for them, and re-layouts: none -> 4.79 us  [the longest x1 2.53 us: on_device(): per_slot_t.transpose(0, 2, 1)]
    ppermute x5, waiting for transfers between devices: 36.7 us -> 40.6 us  [all_sum(): values = values + lax.ppermute(values, name, pairs)]
  transfers between devices with their start and end apart: 10 -> 10, of which waited for: 8 -> 8; matrix products, arithmetic and copies ran while one was open for 2% -> 5% of each run, Pallas kernels for 23% -> 6%
where the time goes in v2:
time: 191 us; the launch traced here: 192 us
  waiting for transfers between devices  104 us (54%)
  Pallas kernels  26.9 us (14%)
  starting transfers between devices  21.2 us (11%)
  between operations  14.9 us (8%)
  local copies, waits for them, and re-layouts  10.5 us (5%)
  other arithmetic  8.38 us (4%)
  matrix products  6.11 us (3%)
    ppermute x5, waiting for transfers between devices, all_sum(): values = values + lax.ppermute(values, name, pairs)  40.6 us
    reduce_scatter x1, waiting for transfers between devices, on_device(): reduced = lax.psum_scatter(packed, 'col', scatter_dimension=0, tiled=True)  30.2 us
    all_gather x1, waiting for transfers between devices, on_device(): adjoint_panel = lax.all_gather(grad_agg, 'col', axis=0, tiled=True)  16.2 us
    pallas_call x1, Pallas kernels, aggregate_forward(): pl.pallas_call(_forward_kernel, grid_spec=grid_spec, out_shape=[jax.Shape...  15.4 us
    pallas_call x1, Pallas kernels, aggregate_backward(): pl.pallas_call(_backward_kernel, grid_spec=grid_spec, out_shape=jax.Shape...  11.4 us
    all_to_all x1, waiting for transfers between devices, on_device(): lax.all_to_all(outgoing, 'row', split_axis=0, concat_axis=0, tiled=True)  11.3 us
    all_to_all x1, starting transfers between devices, on_device(): lax.all_to_all(wanted, 'row', split_axis=0, concat_axis=0, tiled=True)  7.31 us
    ppermute x5, starting transfers between devices, all_sum(): values = values + lax.ppermute(values, name, pairs)  6.65 us
  transfers between devices with their start and end apart: 10, of which 8 were waited for; matrix products, arithmetic and copies ran while one was open for 5% of the time, Pallas kernels for 6%

profile of v2, /device:TPU:0, one launch (start us, length us, event | category | flops | bytes accessed | tf_op | source)
XLA Modules:
  0.0 191.8 jit_solution(11467241471421369674)
XLA Ops:
  7.2 1.4 copy.19
  8.6 7.3 %all-to-all-start = ((s32[8,1,2]{2,1,0:T(1,128)}), s32[8,1,2]{2,1,0:T(1,128)S(1)}, u32[]{:S(2)}, u32[]{:S(2)}) async-start(s32[8,1,2]{2,1,0:T(1,128)} %copy.19), calls=%async_computation | async-start | bytes 8192 | tf_op jit(solution)/shard_map/all_to_all | solution.py:167
  15.9 1.1 reshape_reshape_squeeze.3
  17.0 5.4 %all-to-all-done = s32[8,1,2]{2,1,0:T(1,128)S(1)} async-done(((s32[8,1,2]{2,1,0:T(1,128)}), s32[8,1,2]{2,1,0:T(1,128)S(1)}, u32[]{:S(2)}, u32[]{:S(2)}) %all-to-all-start) | async-done | bytes 96 | tf_op jit(solution)/shard_map/all_to_all | solution.py:167
  23.9 0.9 copy.22
  24.8 3.5 %all-to-all-start.1 = ((bf16[8,2,128,128]{3,2,1,0:T(8,128)(2,1)}), bf16[8,2,128,128]{3,2,1,0:T(8,128)(2,1)S(1)}, u32[]{:S(2)}, u32[]{:S(2)}) async-start(bf16[8,2,128,128]{3,2,1,0:T(8,128)(2,1)} %bitcast.22), calls=%async_computation.1 | async-start | bytes 1048576 | tf_op jit(solution)/shard_map/all_to_all | solution.py:174
  30.2 11.3 %all-to-all-done.1 = bf16[8,2,128,128]{3,2,1,0:T(8,128)(2,1)S(1)} async-done(((bf16[8,2,128,128]{3,2,1,0:T(8,128)(2,1)}), bf16[8,2,128,128]{3,2,1,0:T(8,128)(2,1)S(1)}, u32[]{:S(2)}, u32[]{:S(2)}) %all-to-all-start.1) | async-done | bytes 524320 | tf_op jit(solution)/shard_map/all_to_all | solution.py:174
  41.6 0.8 copy-done.2
  42.4 15.4 %shard_map.137 = (f32[32,128,128]{2,1,0:T(8,128)}, f32[32,8,128]{2,1,0:T(8,128)}) custom-call(s32[1]{0:T(128)} %bitcast.50.count_ref, s32[320]{0:T(512)} %reduce.row_ref, s32[320]{0:T(512)} %reduce.1.slot_ref, bf16[320,128,128]{2,1,0:T(8,128)(2,1)} %bitcast.52, bf16[16,128,128]{2,1,0:T(8,128)(2,1)} %bitcast.58), custom_call_target="tpu_custom_call" | custom-call | flops 1426063360 | bytes 13238272 | tf_op jit(solution)/shard_map/pallas_call | solution.py:102
  57.8 0.9 slice.18
  58.7 3.1 %select_maximum_fusion = f32[4,1040,128]{2,1,0:T(8,128)} fusion(f32[4,8,128]{2,1,0:T(8,128)S(1)} %bitcast.61, f32[4,1024,128]{2,1,0:T(8,128)} %bitcast.59), kind=kLoop, calls=%fused_computation.1 | loop fusion | flops 1597440 | bytes 4243456 | tf_op jit(solution)/shard_map/concatenate | solution.py:182
  62.2 30.2 %reduce-scatter.2.cloned.1.call-done = f32[1040,128]{1,0:T(8,128)} async-done(((f32[4160,128]{1,0:T(8,128)}), f32[1040,128]{1,0:T(8,128)}) %reduce-scatter.2.cloned.1.call-update) | async-done | bytes 532496 | tf_op jit(solution)/shard_map/reduce_scatter | solution.py:184
  92.5 0.7 fusion.23
  93.2 1.2 fusion.18
  94.4 1.9 convert_reduce_fusion
  96.3 1.0 fusion.3
  98.0 16.2 %all-gather.2.cloned.1.call-done = bf16[4096,128]{1,0:T(8,128)(2,1)} async-done(((bf16[1024,128]{1,0:T(8,128)(2,1)}), bf16[4096,128]{1,0:T(8,128)(2,1)}) %all-gather.2.cloned.1.call-update) | async-done | bytes 1048592 | tf_op jit(solution)/shard_map/all_gather | solution.py:214
  114.2 2.3 %copy.20 = bf16[32,128,128]{1,2,0:T(8,128)(2,1)} copy(bf16[32,128,128]{2,1,0:T(8,128)(2,1)} %bitcast.60) | data formatting | bytes 2097152 | tf_op jit(solution)/shard_map/reshape | solution.py:215
  116.5 11.4 %shard_map.138 = f32[16,128,128]{2,1,0:T(8,128)} custom-call(s32[1]{0:T(128)} %bitcast.51.count_ref, s32[320]{0:T(512)} %reduce.row_ref, s32[320]{0:T(512)} %reduce.1.slot_ref, bf16[320,128,128]{2,1,0:T(8,128)(2,1)} %bitcast.53, bf16[32,128,128]{2,1,0:T(8,128)(2,1)} %bitcast.55), custom_call_target="tpu_custom_call" | custom-call | flops 1342177280 | bytes 12582912 | tf_op jit(solution)/shard_map/pallas_call | solution.py:130
  127.9 2.5 %copy.21 = f32[8,2,128,128]{3,2,1,0:T(8,128)} copy(f32[8,2,128,128]{2,3,1,0:T(8,128)} %bitcast.56) | data formatting | bytes 2097152 | tf_op jit(solution)/shard_map/reshape | solution.py:219
  130.4 3.7 %all-to-all-start.2 = ((f32[8,2,128,128]{3,2,1,0:T(8,128)}), f32[8,2,128,128]{3,2,1,0:T(8,128)S(1)}, u32[]{:S(2)}, u32[]{:S(2)}) async-start(f32[8,2,128,128]{3,2,1,0:T(8,128)} %copy.21), calls=%async_computation.3 | async-start | bytes 2097152 | tf_op jit(solution)/shard_map/all_to_all | solution.py:220
  134.2 2.5 %collective-permute-start.1 = (f32[264,256]{1,0:T(8,128)S(1)}, f32[264,256]{1,0:T(8,128)S(1)}, u32[]{:S(2)}, u32[]{:S(2)}) collective-permute-start(f32[264,256]{1,0:T(8,128)S(1)} %fusion.26), channel_id=1, source_target_pairs={{0,2},{1,3},{2,0},{3,1},{4,6},{5,7},{6,4},{7,5},{8,10},{9,11},{10,... | collective-permute-start | bytes 811016 | tf_op jit(solution)/shard_map/ppermute | solution.py:149
  136.6 6.9 %collective-permute-done.1 = f32[264,256]{1,0:T(8,128)S(1)} collective-permute-done((f32[264,256]{1,0:T(8,128)S(1)}, f32[264,256]{1,0:T(8,128)S(1)}, u32[]{:S(2)}, u32[]{:S(2)}) %collective-permute-start.1) | collective-permute-done | bytes 270368 | tf_op jit(solution)/shard_map/ppermute | solution.py:149
  143.5 1.8 collective-permute-start.2
  145.3 10.4 %collective-permute-done.2 = f32[264,256]{1,0:T(8,128)S(1)} collective-permute-done((f32[264,256]{1,0:T(8,128)S(1)}, f32[264,256]{1,0:T(8,128)S(1)}, u32[]{:S(2)}, u32[]{:S(2)}) %collective-permute-start.2) | collective-permute-done | bytes 270368 | tf_op jit(solution)/shard_map/ppermute | solution.py:149
  155.7 1.3 collective-permute-start.3
  157.1 10.2 %collective-permute-done.3 = f32[264,256]{1,0:T(8,128)S(1)} collective-permute-done((f32[264,256]{1,0:T(8,128)S(1)}, f32[264,256]{1,0:T(8,128)S(1)}, u32[]{:S(2)}, u32[]{:S(2)}) %collective-permute-start.3) | collective-permute-done | bytes 270368 | tf_op jit(solution)/shard_map/ppermute | solution.py:149
  167.3 1.0 collective-permute-start.4
  168.3 13.1 %collective-permute-done.4 = f32[264,256]{1,0:T(8,128)S(1)} collective-permute-done((f32[264,256]{1,0:T(8,128)S(1)}, f32[264,256]{1,0:T(8,128)S(1)}, u32[]{:S(2)}, u32[]{:S(2)}) %collective-permute-start.4) | collective-permute-done | bytes 270368 | tf_op jit(solution)/shard_map/ppermute | solution.py:149
  182.1 0.7 slice_multiply_fusion
  182.8 1.1 fusion.15
  183.9 1.0 fusion.4
  (40 shorter events, 4.7 us)
Async XLA Ops:
  7.2 87.2 %copy-start = (bf16[128,256]{1,0:T(8,128)(2,1)S(1)}, bf16[128,256]{1,0:T(8,128)(2,1)}, u32[]{:S(2)}) copy-start(bf16[128,256]{1,0:T(8,128)(2,1)} %param.12) | copy-start | bytes 196612
  7.2 21.2 %copy-start.4 = (s32[1,1,320]{2,1,0:T(1,128)S(1)}, s32[1,1,320]{2,1,0:T(1,128)}, u32[]{:S(2)}) copy-start(s32[1,1,320]{2,1,0:T(1,128)} %param.15) | copy-start | bytes 3844
  7.2 21.8 %copy-start.5 = (s32[1,1,320]{2,1,0:T(1,128)S(1)}, s32[1,1,320]{2,1,0:T(1,128)}, u32[]{:S(2)}) copy-start(s32[1,1,320]{2,1,0:T(1,128)} %param.16) | copy-start | bytes 3844
  8.6 13.7 %all-to-all-start = ((s32[8,1,2]{2,1,0:T(1,128)}), s32[8,1,2]{2,1,0:T(1,128)S(1)}, u32[]{:S(2)}, u32[]{:S(2)}) async-start(s32[8,1,2]{2,1,0:T(1,128)} %copy.19), calls=%async_computation | async-start | bytes 8192 | tf_op jit(solution)/shard_map/all_to_all | solution.py:167
  24.8 16.8 %all-to-all-start.1 = ((bf16[8,2,128,128]{3,2,1,0:T(8,128)(2,1)}), bf16[8,2,128,128]{3,2,1,0:T(8,128)(2,1)S(1)}, u32[]{:S(2)}, u32[]{:S(2)}) async-start(bf16[8,2,128,128]{3,2,1,0:T(8,128)(2,1)} %bitcast.22), calls=%async_computation.1 | async-start | bytes 1048576 | tf_op jit(solution)/shard_map/all_to_all | solution.py:174
  28.3 64.2 %reduce-scatter.2.cloned.1.call-start = ((), (), s32[]{:S(2)}) async-start(), calls=%async_computation.4 | async-start | bytes 2662400 | tf_op jit(solution)/shard_map/reduce_scatter | solution.py:184
  41.6 0.8 copy-start.2
  58.7 3.2 %copy-start.1 = (bf16[1,1024,128]{2,1,0:T(8,128)(2,1)S(1)}, bf16[1,1024,128]{2,1,0:T(8,128)(2,1)}, u32[]{:S(2)}) copy-start(bf16[1,1024,128]{2,1,0:T(8,128)(2,1)} %param.10) | copy-start | bytes 786436
  58.7 3.2 %copy-start.3 = (bf16[128,256]{1,0:T(8,128)(2,1)S(1)}, bf16[128,256]{1,0:T(8,128)(2,1)}, u32[]{:S(2)}) copy-start(bf16[128,256]{1,0:T(8,128)(2,1)} %param.11) | copy-start | bytes 196612
  61.9 32.6 %copy-start.6 = (bf16[1,1024,256]{2,1,0:T(8,128)(2,1)S(1)}, bf16[1,1024,256]{2,1,0:T(8,128)(2,1)}, u32[]{:S(2)}) copy-start(bf16[1,1024,256]{2,1,0:T(8,128)(2,1)} %param.19) | copy-start | bytes 1572868
  61.9 32.6 %copy-start.7 = (f32[256]{0:T(256)S(1)}, f32[256]{0:T(256)}, u32[]{:S(2)}) copy-start(f32[256]{0:T(256)} %param.13) | copy-start | bytes 3076
  61.9 52.3 %all-gather.2.cloned.1.call-start = ((), (), s32[]{:S(2)}) async-start(), calls=%async_computation.5 | async-start | bytes 1310720 | tf_op jit(solution)/shard_map/all_gather | solution.py:214
  97.9 36.2 %collective-permute-start = (f32[264,256]{1,0:T(8,128)S(1)}, f32[264,256]{1,0:T(8,128)S(1)}, u32[]{:S(2)}, u32[]{:S(2)}) collective-permute-start(f32[264,256]{1,0:T(8,128)S(1)} %pad_maximum_fusion), channel_id=1, source_target_pairs={{0,1},{1,0},{2,3},{3,2},{4,5},{5,4},{6,7},{7,6},{8,9},{9,8},{10,11... | collective-permute-start | bytes 811016 | tf_op jit(solution)/shard_map/ppermute | solution.py:149
  130.4 52.4 %all-to-all-start.2 = ((f32[8,2,128,128]{3,2,1,0:T(8,128)}), f32[8,2,128,128]{3,2,1,0:T(8,128)S(1)}, u32[]{:S(2)}, u32[]{:S(2)}) async-start(f32[8,2,128,128]{3,2,1,0:T(8,128)} %copy.21), calls=%async_computation.3 | async-start | bytes 2097152 | tf_op jit(solution)/shard_map/all_to_all | solution.py:220
  134.2 9.3 %collective-permute-start.1 = (f32[264,256]{1,0:T(8,128)S(1)}, f32[264,256]{1,0:T(8,128)S(1)}, u32[]{:S(2)}, u32[]{:S(2)}) collective-permute-start(f32[264,256]{1,0:T(8,128)S(1)} %fusion.26), channel_id=1, source_target_pairs={{0,2},{1,3},{2,0},{3,1},{4,6},{5,7},{6,4},{7,5},{8,10},{9,11},{10,... | collective-permute-start | bytes 811016 | tf_op jit(solution)/shard_map/ppermute | solution.py:149
  143.5 12.2 %collective-permute-start.2 = (f32[264,256]{1,0:T(8,128)S(1)}, f32[264,256]{1,0:T(8,128)S(1)}, u32[]{:S(2)}, u32[]{:S(2)}) collective-permute-start(f32[264,256]{1,0:T(8,128)S(1)} %add.63), channel_id=1, source_target_pairs={{0,4},{4,0},{8,12},{12,8},{16,20},{20,16},{24,28},{28,24},{1,5},{5... | collective-permute-start | bytes 811016 | tf_op jit(solution)/shard_map/ppermute | solution.py:149
  155.7 11.5 %collective-permute-start.3 = (f32[264,256]{1,0:T(8,128)S(1)}, f32[264,256]{1,0:T(8,128)S(1)}, u32[]{:S(2)}, u32[]{:S(2)}) collective-permute-start(f32[264,256]{1,0:T(8,128)S(1)} %add.64), channel_id=1, source_target_pairs={{0,8},{4,12},{8,0},{12,4},{16,24},{20,28},{24,16},{28,20},{1,9},{5... | collective-permute-start | bytes 811016 | tf_op jit(solution)/shard_map/ppermute | solution.py:149
  167.3 14.1 %collective-permute-start.4 = (f32[264,256]{1,0:T(8,128)S(1)}, f32[264,256]{1,0:T(8,128)S(1)}, u32[]{:S(2)}, u32[]{:S(2)}) collective-permute-start(f32[264,256]{1,0:T(8,128)S(1)} %add.65), channel_id=1, source_target_pairs={{0,16},{4,20},{8,24},{12,28},{16,0},{20,4},{24,8},{28,12},{1,17},{... | collective-permute-start | bytes 811016 | tf_op jit(solution)/shard_map/ppermute | solution.py:149
Sparse Core Ops, SparseCore 0:
  62.0 30.4 reduce-scatter.1
  97.5 16.7 all-gather.1

commit v3 on v2

--- a/solution.py
+++ b/solution.py
@@ -140,15 +140,21 @@
     )(counts, rows, slots, blocks, grad_panel)
 
 
-def all_sum(values, axes):
+def exchange_steps(axes):
+    steps = []
     for name in axes:
         size = lax.axis_size(name)
         step = 1
         while step < size:
-            pairs = [(i, i ^ step) for i in range(size)]
-            values = values + lax.ppermute(values, name, pairs)
+            steps.append((name, size, step))
             step *= 2
-    return values
+    return steps[::-1]
+
+
+def exchange_add(values, step):
+    name, size, offset = step
+    pairs = [(i, i ^ offset) for i in range(size)]
+    return values + lax.ppermute(values, name, pairs)
 
 
 def on_device(
@@ -201,32 +207,40 @@
     weight_pack = jnp.concatenate(
         [local_self, local_neigh, jnp.broadcast_to(local_bias[None], (8, hid))], axis=0
     )
-    weight_pack = all_sum(weight_pack, ("col", "row"))
+    steps = exchange_steps(("col", "row"))
+    grad_agg = (
+        jnp.einsum("nh,dh->nd", grad_round, w_neigh, preferred_element_type=jnp.float32)
+        / divisor[:, None]
+    )
+    grad_agg = grad_agg.astype(jnp.bfloat16)
+    adjoint_panel = lax.all_gather(grad_agg, "col", axis=0, tiled=True)
+    weight_pack = exchange_add(weight_pack, steps[0])
+    weight_pack, adjoint_panel = lax.optimization_barrier((weight_pack, adjoint_panel))
+    panel_t = adjoint_panel.reshape(panel_blocks, block_size, feat_width).transpose(0, 2, 1)
+    per_slot_t = aggregate_backward(
+        live_count, block_rows, block_slots, blocks[0, 0], panel_t, fetch_total
+    )
+    weight_pack = exchange_add(weight_pack, steps[1])
+    weight_pack, per_slot_t = lax.optimization_barrier((weight_pack, per_slot_t))
+    per_slot = per_slot_t.transpose(0, 2, 1).reshape(row_count, picks_each, block_size, feat_width)
+    returned = lax.all_to_all(per_slot, "row", split_axis=0, concat_axis=0, tiled=True)
+    weight_pack = exchange_add(weight_pack, steps[2])
+    weight_pack, returned = lax.optimization_barrier((weight_pack, returned))
+    incoming = group_rows(
+        asked_for.reshape(-1),
+        returned.reshape(fetch_total, block_size, feat_width),
+        owned_count,
+    )
+    incoming = incoming.reshape(node_count, feat_width)
+    grad_feats = (
+        jnp.einsum("nh,dh->nd", grad_round, w_self, preferred_element_type=jnp.float32) + incoming
+    )
+    for step in steps[3:]:
+        weight_pack = exchange_add(weight_pack, step)
     factor = 1.0 / math.sqrt(node_count * row_count * col_count)
     grad_self = weight_pack[:feat_width] * factor
     grad_neigh = weight_pack[feat_width : 2 * feat_width] * factor
     grad_bias = weight_pack[2 * feat_width] * factor
-    grad_agg = (
-        jnp.einsum("nh,dh->nd", grad_round, w_neigh, preferred_element_type=jnp.float32)
-        / divisor[:, None]
-    )
-    grad_agg = grad_agg.astype(jnp.bfloat16)
-    adjoint_panel = lax.all_gather(grad_agg, "col", axis=0, tiled=True)
-    panel_t = adjoint_panel.reshape(panel_blocks, block_size, feat_width).transpose(0, 2, 1)
-    per_slot_t = aggregate_backward(
-        live_count, block_rows, block_slots, blocks[0, 0], panel_t, fetch_total
-    )
-    per_slot = per_slot_t.transpose(0, 2, 1).reshape(row_count, picks_each, block_size, feat_width)
-    returned = lax.all_to_all(per_slot, "row", split_axis=0, concat_axis=0, tiled=True)
-    incoming = group_rows(
-        asked_for.reshape(-1),
-        returned.reshape(fetch_total, block_size, feat_width),
-        owned_count,
-    )
-    incoming = incoming.reshape(node_count, feat_width)
-    grad_feats = (
-        jnp.einsum("nh,dh->nd", grad_round, w_self, preferred_element_type=jnp.float32) + incoming
-    )
     return (
         output.astype(jnp.bfloat16)[None],
         grad_feats.astype(jnp.bfloat16)[None],

time: 191 us -> 178 us (0.932)
  waiting for transfers between devices: 104 us -> 90 us
    all_gather x1, waiting for transfers between devices: 16.2 us -> 1.43 us  [on_device(): adjoint_panel = lax.all_gather(grad_agg, 'col', axis=0, tiled=True)]
    all_to_all x1, waiting for transfers between devices: 0.01 us -> 7.93 us  [on_device(): lax.all_to_all(per_slot, 'row', split_axis=0, concat_axis=0, tiled=True)]
    ppermute x5, waiting for transfers between devices: 40.6 us -> 34.9 us  [exchange_add(): return values + lax.ppermute(values, name, pairs)]
  transfers between devices with their start and end apart: 10 -> 10, of which waited for: 8 -> 8; matrix products, arithmetic and copies ran while one was open for 5% -> 4% of each run, Pallas kernels for 6% -> 6%
where the time goes in v3:
time: 178 us; the launch traced here: 179 us
  waiting for transfers between devices  90 us (51%)
  Pallas kernels  26.9 us (15%)
  starting transfers between devices  21.8 us (12%)
  between operations  14.9 us (8%)
  local copies, waits for them, and re-layouts  10.5 us (6%)
  other arithmetic  8.39 us (5%)
  matrix products  6.1 us (3%)
    ppermute x5, waiting for transfers between devices, exchange_add(): return values + lax.ppermute(values, name, pairs)  34.9 us
    reduce_scatter x1, waiting for transfers between devices, on_device(): reduced = lax.psum_scatter(packed, 'col', scatter_dimension=0, tiled=True)  29.1 us
    pallas_call x1, Pallas kernels, aggregate_forward(): pl.pallas_call(_forward_kernel, grid_spec=grid_spec, out_shape=[jax.Shape...  15.4 us
    pallas_call x1, Pallas kernels, aggregate_backward(): pl.pallas_call(_backward_kernel, grid_spec=grid_spec, out_shape=jax.Shape...  11.4 us
    all_to_all x1, waiting for transfers between devices, on_device(): lax.all_to_all(outgoing, 'row', split_axis=0, concat_axis=0, tiled=True)  11.3 us
    all_to_all x1, waiting for transfers between devices, on_device(): lax.all_to_all(per_slot, 'row', split_axis=0, concat_axis=0, tiled=True)  7.93 us
    ppermute x5, starting transfers between devices, exchange_add(): return values + lax.ppermute(values, name, pairs)  7.36 us
    all_to_all x1, starting transfers between devices, on_device(): lax.all_to_all(wanted, 'row', split_axis=0, concat_axis=0, tiled=True)  7.31 us
  transfers between devices with their start and end apart: 10, of which 8 were waited for; matrix products, arithmetic and copies ran while one was open for 4% of the time, Pallas kernels for 6%

profile of v3, /device:TPU:0, one launch (start us, length us, event | category | flops | bytes accessed | tf_op | source)
XLA Modules:
  0.0 178.6 jit_solution(4090859378670884954)
XLA Ops:
  7.2 1.4 copy.19
  8.6 7.3 %all-to-all-start = ((s32[8,1,2]{2,1,0:T(1,128)}), s32[8,1,2]{2,1,0:T(1,128)S(1)}, u32[]{:S(2)}, u32[]{:S(2)}) async-start(s32[8,1,2]{2,1,0:T(1,128)} %copy.19), calls=%async_computation | async-start | bytes 8192 | tf_op jit(solution)/shard_map/all_to_all | solution.py:173
  15.9 1.1 reshape_reshape_squeeze.3
  17.0 5.4 %all-to-all-done = s32[8,1,2]{2,1,0:T(1,128)S(1)} async-done(((s32[8,1,2]{2,1,0:T(1,128)}), s32[8,1,2]{2,1,0:T(1,128)S(1)}, u32[]{:S(2)}, u32[]{:S(2)}) %all-to-all-start) | async-done | bytes 96 | tf_op jit(solution)/shard_map/all_to_all | solution.py:173
  23.9 0.9 copy.22
  24.8 3.5 %all-to-all-start.1 = ((bf16[8,2,128,128]{3,2,1,0:T(8,128)(2,1)}), bf16[8,2,128,128]{3,2,1,0:T(8,128)(2,1)S(1)}, u32[]{:S(2)}, u32[]{:S(2)}) async-start(bf16[8,2,128,128]{3,2,1,0:T(8,128)(2,1)} %bitcast.22), calls=%async_computation.1 | async-start | bytes 1048576 | tf_op jit(solution)/shard_map/all_to_all | solution.py:180
  30.2 11.3 %all-to-all-done.1 = bf16[8,2,128,128]{3,2,1,0:T(8,128)(2,1)S(1)} async-done(((bf16[8,2,128,128]{3,2,1,0:T(8,128)(2,1)}), bf16[8,2,128,128]{3,2,1,0:T(8,128)(2,1)S(1)}, u32[]{:S(2)}, u32[]{:S(2)}) %all-to-all-start.1) | async-done | bytes 524320 | tf_op jit(solution)/shard_map/all_to_all | solution.py:180
  41.6 0.8 copy-done.2
  42.4 15.4 %shard_map.137 = (f32[32,128,128]{2,1,0:T(8,128)}, f32[32,8,128]{2,1,0:T(8,128)}) custom-call(s32[1]{0:T(128)} %bitcast.50.count_ref, s32[320]{0:T(512)} %reduce.row_ref, s32[320]{0:T(512)} %reduce.1.slot_ref, bf16[320,128,128]{2,1,0:T(8,128)(2,1)} %bitcast.52, bf16[16,128,128]{2,1,0:T(8,128)(2,1)} %bitcast.58), custom_call_target="tpu_custom_call" | custom-call | flops 1426063360 | bytes 13238272 | tf_op jit(solution)/shard_map/pallas_call | solution.py:102
  57.8 0.9 slice.18
  58.7 3.1 %select_maximum_fusion = f32[4,1040,128]{2,1,0:T(8,128)} fusion(f32[4,8,128]{2,1,0:T(8,128)S(1)} %bitcast.61, f32[4,1024,128]{2,1,0:T(8,128)} %bitcast.59), kind=kLoop, calls=%fused_computation.1 | loop fusion | flops 1597440 | bytes 4243456 | tf_op jit(solution)/shard_map/concatenate | solution.py:188
  62.2 29.1 %reduce-scatter.2.cloned.1.call-done = f32[1040,128]{1,0:T(8,128)} async-done(((f32[4160,128]{1,0:T(8,128)}), f32[1040,128]{1,0:T(8,128)}) %reduce-scatter.2.cloned.1.call-update) | async-done | bytes 532496 | tf_op jit(solution)/shard_map/reduce_scatter | solution.py:190
  91.3 0.7 fusion.23
  92.0 1.2 fusion.18
  93.3 1.9 %convert_reduce_fusion = (f32[256]{0:T(256)S(1)}, bf16[1024,256]{1,0:T(8,128)(2,1)S(1)}, bf16[1,1024,256]{2,1,0:T(8,128)(2,1)}) fusion(bf16[1,1024,256]{2,1,0:T(8,128)(2,1)S(1)} %copy-done.6, f32[256]{0:T(256)S(1)} %copy-done.7, f32[1024,256]{1,0:T(8,128)S(1)} %fusion.21, bf16[1024,128]{1,0:T(8,128)(2,1)S(1)} %fusion.18, bf16[128,256]{1,0:T(8,128)(2,1)S(1)} %copy-done), kind=kOutput, calls=%fused_computation.29 | convolution fusion | flops 74186496 | bytes 2951168 | tf_op jit(solution)/shard_map/dot_general | solution.py:197
  95.1 1.0 fusion.3
  96.8 2.4 %collective-permute-start = (f32[264,256]{1,0:T(8,128)S(1)}, f32[264,256]{1,0:T(8,128)S(1)}, u32[]{:S(2)}, u32[]{:S(2)}) collective-permute-start(f32[264,256]{1,0:T(8,128)S(1)} %pad_maximum_fusion), channel_id=1, source_target_pairs={{0,16},{4,20},{8,24},{12,28},{16,0},{20,4},{24,8},{28,12},{1,17},{... | collective-permute-start | bytes 811016 | tf_op jit(solution)/shard_map/ppermute | solution.py:157
  99.2 12.3 %collective-permute-done = f32[264,256]{1,0:T(8,128)S(1)} collective-permute-done((f32[264,256]{1,0:T(8,128)S(1)}, f32[264,256]{1,0:T(8,128)S(1)}, u32[]{:S(2)}, u32[]{:S(2)}) %collective-permute-start) | collective-permute-done | bytes 270368 | tf_op jit(solution)/shard_map/ppermute | solution.py:157
  111.6 1.4 all-gather.2.cloned.1.call-done
  113.0 1.5 collective-permute-start.1
  114.5 2.3 %copy.20 = bf16[32,128,128]{1,2,0:T(8,128)(2,1)} copy(bf16[32,128,128]{2,1,0:T(8,128)(2,1)} %bitcast.60) | data formatting | bytes 2097152 | tf_op jit(solution)/shard_map/reshape | solution.py:219
  116.8 11.4 %shard_map.138 = f32[16,128,128]{2,1,0:T(8,128)} custom-call(s32[1]{0:T(128)} %bitcast.51.count_ref, s32[320]{0:T(512)} %reduce.row_ref, s32[320]{0:T(512)} %reduce.1.slot_ref, bf16[320,128,128]{2,1,0:T(8,128)(2,1)} %bitcast.53, bf16[32,128,128]{2,1,0:T(8,128)(2,1)} %bitcast.56), custom_call_target="tpu_custom_call" | custom-call | flops 1342177280 | bytes 12582912 | tf_op jit(solution)/shard_map/pallas_call | solution.py:130
  128.2 2.5 %copy.21 = f32[8,2,128,128]{3,2,1,0:T(8,128)} copy(f32[8,2,128,128]{2,3,1,0:T(8,128)} %bitcast.55) | data formatting | bytes 2097152 | tf_op jit(solution)/shard_map/reshape | solution.py:225
  130.8 3.6 %all-to-all-start.2 = ((f32[8,2,128,128]{3,2,1,0:T(8,128)}), f32[8,2,128,128]{3,2,1,0:T(8,128)S(1)}, u32[]{:S(2)}, u32[]{:S(2)}) async-start(f32[8,2,128,128]{3,2,1,0:T(8,128)} %copy.21), calls=%async_computation.3 | async-start | bytes 2097152 | tf_op jit(solution)/shard_map/all_to_all | solution.py:226
  134.3 1.9 %collective-permute-start.2 = (f32[264,256]{1,0:T(8,128)S(1)}, f32[264,256]{1,0:T(8,128)S(1)}, u32[]{:S(2)}, u32[]{:S(2)}) collective-permute-start(f32[264,256]{1,0:T(8,128)S(1)} %add.62), channel_id=1, source_target_pairs={{0,4},{4,0},{8,12},{12,8},{16,20},{20,16},{24,28},{28,24},{1,5},{5... | collective-permute-start | bytes 811016 | tf_op jit(solution)/shard_map/ppermute | solution.py:157
  136.3 15.6 %collective-permute-done.2 = f32[264,256]{1,0:T(8,128)S(1)} collective-permute-done((f32[264,256]{1,0:T(8,128)S(1)}, f32[264,256]{1,0:T(8,128)S(1)}, u32[]{:S(2)}, u32[]{:S(2)}) %collective-permute-start.2) | collective-permute-done | bytes 270368 | tf_op jit(solution)/shard_map/ppermute | solution.py:157
  151.9 7.9 %all-to-all-done.2 = f32[8,2,128,128]{3,2,1,0:T(8,128)S(1)} async-done(((f32[8,2,128,128]{3,2,1,0:T(8,128)}), f32[8,2,128,128]{3,2,1,0:T(8,128)S(1)}, u32[]{:S(2)}, u32[]{:S(2)}) %all-to-all-start.2) | async-done | bytes 1048608 | tf_op jit(solution)/shard_map/all_to_all | solution.py:226
  159.8 1.4 collective-permute-start.3
  161.3 6.9 %collective-permute-done.3 = f32[264,256]{1,0:T(8,128)S(1)} collective-permute-done((f32[264,256]{1,0:T(8,128)S(1)}, f32[264,256]{1,0:T(8,128)S(1)}, u32[]{:S(2)}, u32[]{:S(2)}) %collective-permute-start.3) | collective-permute-done | bytes 270368 | tf_op jit(solution)/shard_map/ppermute | solution.py:157
  168.3 1.1 fusion.15
  169.4 1.0 fusion.4
  170.5 0.7 slice_multiply_fusion
  (40 shorter events, 4.7 us)
Async XLA Ops:
  7.2 86.1 %copy-start = (bf16[128,256]{1,0:T(8,128)(2,1)S(1)}, bf16[128,256]{1,0:T(8,128)(2,1)}, u32[]{:S(2)}) copy-start(bf16[128,256]{1,0:T(8,128)(2,1)} %param.12) | copy-start | bytes 196612
  7.2 21.2 %copy-start.4 = (s32[1,1,320]{2,1,0:T(1,128)S(1)}, s32[1,1,320]{2,1,0:T(1,128)}, u32[]{:S(2)}) copy-start(s32[1,1,320]{2,1,0:T(1,128)} %param.15) | copy-start | bytes 3844
  7.2 21.8 %copy-start.5 = (s32[1,1,320]{2,1,0:T(1,128)S(1)}, s32[1,1,320]{2,1,0:T(1,128)}, u32[]{:S(2)}) copy-start(s32[1,1,320]{2,1,0:T(1,128)} %param.16) | copy-start | bytes 3844
  8.6 13.7 %all-to-all-start = ((s32[8,1,2]{2,1,0:T(1,128)}), s32[8,1,2]{2,1,0:T(1,128)S(1)}, u32[]{:S(2)}, u32[]{:S(2)}) async-start(s32[8,1,2]{2,1,0:T(1,128)} %copy.19), calls=%async_computation | async-start | bytes 8192 | tf_op jit(solution)/shard_map/all_to_all | solution.py:173
  24.8 16.8 %all-to-all-start.1 = ((bf16[8,2,128,128]{3,2,1,0:T(8,128)(2,1)}), bf16[8,2,128,128]{3,2,1,0:T(8,128)(2,1)S(1)}, u32[]{:S(2)}, u32[]{:S(2)}) async-start(bf16[8,2,128,128]{3,2,1,0:T(8,128)(2,1)} %bitcast.22), calls=%async_computation.1 | async-start | bytes 1048576 | tf_op jit(solution)/shard_map/all_to_all | solution.py:180
  28.3 63.0 %reduce-scatter.2.cloned.1.call-start = ((), (), s32[]{:S(2)}) async-start(), calls=%async_computation.4 | async-start | bytes 2662400 | tf_op jit(solution)/shard_map/reduce_scatter | solution.py:190
  41.6 0.8 copy-start.2
  58.7 3.2 %copy-start.1 = (bf16[1,1024,128]{2,1,0:T(8,128)(2,1)S(1)}, bf16[1,1024,128]{2,1,0:T(8,128)(2,1)}, u32[]{:S(2)}) copy-start(bf16[1,1024,128]{2,1,0:T(8,128)(2,1)} %param.10) | copy-start | bytes 786436
  58.7 3.2 %copy-start.3 = (bf16[128,256]{1,0:T(8,128)(2,1)S(1)}, bf16[128,256]{1,0:T(8,128)(2,1)}, u32[]{:S(2)}) copy-start(bf16[128,256]{1,0:T(8,128)(2,1)} %param.11) | copy-start | bytes 196612
  61.9 31.4 %copy-start.6 = (bf16[1,1024,256]{2,1,0:T(8,128)(2,1)S(1)}, bf16[1,1024,256]{2,1,0:T(8,128)(2,1)}, u32[]{:S(2)}) copy-start(bf16[1,1024,256]{2,1,0:T(8,128)(2,1)} %param.19) | copy-start | bytes 1572868
  61.9 31.4 %copy-start.7 = (f32[256]{0:T(256)S(1)}, f32[256]{0:T(256)}, u32[]{:S(2)}) copy-start(f32[256]{0:T(256)} %param.13) | copy-start | bytes 3076
  61.9 51.1 %all-gather.2.cloned.1.call-start = ((), (), s32[]{:S(2)}) async-start(), calls=%async_computation.5 | async-start | bytes 1310720 | tf_op jit(solution)/shard_map/all_gather | solution.py:216
  96.8 14.8 %collective-permute-start = (f32[264,256]{1,0:T(8,128)S(1)}, f32[264,256]{1,0:T(8,128)S(1)}, u32[]{:S(2)}, u32[]{:S(2)}) collective-permute-start(f32[264,256]{1,0:T(8,128)S(1)} %pad_maximum_fusion), channel_id=1, source_target_pairs={{0,16},{4,20},{8,24},{12,28},{16,0},{20,4},{24,8},{28,12},{1,17},{... | collective-permute-start | bytes 811016 | tf_op jit(solution)/shard_map/ppermute | solution.py:157
  113.0 15.2 %collective-permute-start.1 = (f32[264,256]{1,0:T(8,128)S(1)}, f32[264,256]{1,0:T(8,128)S(1)}, u32[]{:S(2)}, u32[]{:S(2)}) collective-permute-start(f32[264,256]{1,0:T(8,128)S(1)} %fusion.26), channel_id=1, source_target_pairs={{0,8},{4,12},{8,0},{12,4},{16,24},{20,28},{24,16},{28,20},{1,9},{5... | collective-permute-start | bytes 811016 | tf_op jit(solution)/shard_map/ppermute | solution.py:157
  130.8 29.0 %all-to-all-start.2 = ((f32[8,2,128,128]{3,2,1,0:T(8,128)}), f32[8,2,128,128]{3,2,1,0:T(8,128)S(1)}, u32[]{:S(2)}, u32[]{:S(2)}) async-start(f32[8,2,128,128]{3,2,1,0:T(8,128)} %copy.21), calls=%async_computation.3 | async-start | bytes 2097152 | tf_op jit(solution)/shard_map/all_to_all | solution.py:226
  134.3 17.5 %collective-permute-start.2 = (f32[264,256]{1,0:T(8,128)S(1)}, f32[264,256]{1,0:T(8,128)S(1)}, u32[]{:S(2)}, u32[]{:S(2)}) collective-permute-start(f32[264,256]{1,0:T(8,128)S(1)} %add.62), channel_id=1, source_target_pairs={{0,4},{4,0},{8,12},{12,8},{16,20},{20,16},{24,28},{28,24},{1,5},{5... | collective-permute-start | bytes 811016 | tf_op jit(solution)/shard_map/ppermute | solution.py:157
  159.8 8.4 %collective-permute-start.3 = (f32[264,256]{1,0:T(8,128)S(1)}, f32[264,256]{1,0:T(8,128)S(1)}, u32[]{:S(2)}, u32[]{:S(2)}) collective-permute-start(f32[264,256]{1,0:T(8,128)S(1)} %add.63), channel_id=1, source_target_pairs={{0,2},{1,3},{2,0},{3,1},{4,6},{5,7},{6,4},{7,5},{8,10},{9,11},{10,... | collective-permute-start | bytes 811016 | tf_op jit(solution)/shard_map/ppermute | solution.py:157
  168.2 2.2 %collective-permute-start.4 = (f32[264,256]{1,0:T(8,128)S(1)}, f32[264,256]{1,0:T(8,128)S(1)}, u32[]{:S(2)}, u32[]{:S(2)}) collective-permute-start(f32[264,256]{1,0:T(8,128)S(1)} %add.65), channel_id=1, source_target_pairs={{0,1},{1,0},{2,3},{3,2},{4,5},{5,4},{6,7},{7,6},{8,9},{9,8},{10,11... | collective-permute-start | bytes 811016 | tf_op jit(solution)/shard_map/ppermute | solution.py:157
Sparse Core Ops, SparseCore 0:
  62.0 29.2 reduce-scatter.1
  96.3 16.6 all-gather.1

commit v4 on v3

--- a/solution.py
+++ b/solution.py
@@ -9,6 +9,7 @@
 from jax.sharding import PartitionSpec as P
 
 GROUP = 32
+DEGREE_ROWS = 16
 
 
 def gelu_tanh(values):
@@ -35,39 +36,41 @@
     return jnp.minimum(g, (count_ref[0] - 1) // GROUP)
 
 
-def _forward_kernel(count_ref, row_ref, slot_ref, blk_ref, feat_ref, sum_ref, deg_ref):
+def _forward_kernel(count_ref, row_ref, slot_ref, blk_ref, feat_ref, deg_ref, out_ref):
     g = pl.program_id(0)
+    bs = blk_ref.shape[-1]
+    node_count = out_ref.shape[1] - deg_ref.shape[1]
+    owned = node_count // bs
 
     @pl.when(g == 0)
     def _():
-        sum_ref[...] = jnp.zeros_like(sum_ref)
-        deg_ref[...] = jnp.zeros_like(deg_ref)
+        out_ref[:, :node_count, :] = jnp.zeros(
+            (out_ref.shape[0], node_count, out_ref.shape[2]), jnp.float32
+        )
+        out_ref[:, node_count:, :] = deg_ref[...]
 
     count = count_ref[0]
-    ones = jnp.ones((8, blk_ref.shape[-1]), jnp.bfloat16)
 
     @pl.when(g * GROUP < count)
     def _():
         for j in range(GROUP):
             k = g * GROUP + j
             live = k < count
-            blk = blk_ref[j]
             r = row_ref[k]
             s = slot_ref[k]
-            prod = jnp.dot(blk, feat_ref[s], preferred_element_type=jnp.float32)
-            rsum = lax.dot_general(
-                ones, blk, (((1,), (1,)), ((), ())), preferred_element_type=jnp.float32
-            )
-            sum_ref[r] += jnp.where(live, prod, 0.0)
-            deg_ref[r] += jnp.where(live, rsum, 0.0)
-
-
-def _backward_kernel(count_ref, row_ref, slot_ref, blk_ref, grad_ref, out_ref):
+            at = pl.multiple_of((r % owned) * bs, bs)
+            prod = jnp.dot(blk_ref[j], feat_ref[s], preferred_element_type=jnp.float32)
+            out_ref[r // owned, pl.ds(at, bs), :] += jnp.where(live, prod, 0.0)
+
+
+def _backward_kernel(count_ref, row_ref, slot_ref, blk_ref, grad_ref, out_ref, gt_ref, acc_ref):
     g = pl.program_id(0)
 
     @pl.when(g == 0)
     def _():
-        out_ref[...] = jnp.zeros_like(out_ref)
+        for r in range(grad_ref.shape[0]):
+            gt_ref[r] = grad_ref[r].T
+        acc_ref[...] = jnp.zeros_like(acc_ref)
 
     count = count_ref[0]
 
@@ -76,61 +79,65 @@
         for j in range(GROUP):
             k = g * GROUP + j
             live = k < count
-            blk = blk_ref[j]
             r = row_ref[k]
             s = slot_ref[k]
-            prod = jnp.dot(grad_ref[r], blk, preferred_element_type=jnp.float32)
-            out_ref[s] += jnp.where(live, prod, 0.0)
-
-
-def aggregate_forward(counts, rows, slots, blocks, fetched, panel_blocks):
+            prod = jnp.dot(gt_ref[r], blk_ref[j], preferred_element_type=jnp.float32)
+            acc_ref[s] += jnp.where(live, prod, 0.0)
+
+    @pl.when(g == pl.num_programs(0) - 1)
+    def _():
+        for s in range(out_ref.shape[0]):
+            out_ref[s] = acc_ref[s].T
+
+
+def aggregate_forward(counts, rows, slots, blocks, fetched, degree_rows, node_count):
     slot_total, bs, _ = blocks.shape
     fetch_total, _, width = fetched.shape
+    chunks, pad, _ = degree_rows.shape
+    out_rows = node_count + pad
     grid_spec = pltpu.PrefetchScalarGridSpec(
         num_scalar_prefetch=3,
         grid=(slot_total // GROUP,),
         in_specs=[
             pl.BlockSpec((GROUP, bs, bs), lambda g, c, r, s: (_live_group(g, c), 0, 0)),
             pl.BlockSpec((fetch_total, bs, width), lambda g, c, r, s: (0, 0, 0)),
+            pl.BlockSpec((chunks, pad, width), lambda g, c, r, s: (0, 0, 0)),
         ],
-        out_specs=[
-            pl.BlockSpec((panel_blocks, bs, width), lambda g, c, r, s: (0, 0, 0)),
-            pl.BlockSpec((panel_blocks, 8, bs), lambda g, c, r, s: (0, 0, 0)),
-        ],
-    )
-    flops = 2 * slot_total * bs * bs * (width + 8)
+        out_specs=pl.BlockSpec((chunks, out_rows, width), lambda g, c, r, s: (0, 0, 0)),
+    )
     return pl.pallas_call(
         _forward_kernel,
         grid_spec=grid_spec,
-        out_shape=[
-            jax.ShapeDtypeStruct((panel_blocks, bs, width), jnp.float32),
-            jax.ShapeDtypeStruct((panel_blocks, 8, bs), jnp.float32),
-        ],
+        out_shape=jax.ShapeDtypeStruct((chunks, out_rows, width), jnp.float32),
         compiler_params=pltpu.CompilerParams(dimension_semantics=("arbitrary",)),
         cost_estimate=pl.CostEstimate(
-            flops=flops,
-            bytes_accessed=blocks.size * 2 + fetched.size * 2 + panel_blocks * bs * (width + 8) * 4,
+            flops=2 * slot_total * bs * bs * width,
+            bytes_accessed=blocks.size * 2 + fetched.size * 2 + chunks * out_rows * width * 4,
             transcendentals=0,
         ),
-    )(counts, rows, slots, blocks, fetched)
+    )(counts, rows, slots, blocks, fetched, degree_rows)
 
 
 def aggregate_backward(counts, rows, slots, blocks, grad_panel, fetch_total):
     slot_total, bs, _ = blocks.shape
-    panel_blocks, width, _ = grad_panel.shape
+    panel_blocks, _, width = grad_panel.shape
     grid_spec = pltpu.PrefetchScalarGridSpec(
         num_scalar_prefetch=3,
         grid=(slot_total // GROUP,),
         in_specs=[
             pl.BlockSpec((GROUP, bs, bs), lambda g, c, r, s: (_live_group(g, c), 0, 0)),
-            pl.BlockSpec((panel_blocks, width, bs), lambda g, c, r, s: (0, 0, 0)),
+            pl.BlockSpec((panel_blocks, bs, width), lambda g, c, r, s: (0, 0, 0)),
         ],
-        out_specs=pl.BlockSpec((fetch_total, width, bs), lambda g, c, r, s: (0, 0, 0)),
+        out_specs=pl.BlockSpec((fetch_total, bs, width), lambda g, c, r, s: (0, 0, 0)),
+        scratch_shapes=[
+            pltpu.VMEM((panel_blocks, width, bs), jnp.bfloat16),
+            pltpu.VMEM((fetch_total, width, bs), jnp.float32),
+        ],
     )
     return pl.pallas_call(
         _backward_kernel,
         grid_spec=grid_spec,
-        out_shape=jax.ShapeDtypeStruct((fetch_total, width, bs), jnp.float32),
+        out_shape=jax.ShapeDtypeStruct((fetch_total, bs, width), jnp.float32),
         compiler_params=pltpu.CompilerParams(dimension_semantics=("arbitrary",)),
         cost_estimate=pl.CostEstimate(
             flops=2 * slot_total * bs * bs * width,
@@ -179,14 +186,19 @@
     outgoing = outgoing.reshape(row_count, picks_each, block_size, feat_width)
     arrived = lax.all_to_all(outgoing, "row", split_axis=0, concat_axis=0, tiled=True)
     fetched = arrived.reshape(fetch_total, block_size, feat_width)
-    part_sums, part_deg = aggregate_forward(
-        live_count, block_rows, block_slots, blocks[0, 0], fetched, panel_blocks
-    )
-    part_sums = part_sums.reshape(col_count, node_count, feat_width)
-    part_deg = part_deg[:, 0, :].reshape(col_count, owned_count, block_size)
-    part_deg = jnp.pad(part_deg, ((0, 0), (0, 16 - owned_count), (0, 0)))
-    packed = jnp.concatenate([part_sums, part_deg], axis=1)
-    packed = packed.reshape(col_count * (node_count + 16), feat_width)
+    adjacency = blocks[0, 0]
+    live_rows = jnp.where(
+        (jnp.arange(adjacency.shape[0]) < live_count[0])[:, None],
+        jnp.sum(adjacency, axis=2, dtype=jnp.float32),
+        0.0,
+    )
+    part_deg = group_rows(block_rows, live_rows, panel_blocks)
+    part_deg = part_deg.reshape(col_count, owned_count, block_size)
+    part_deg = jnp.pad(part_deg, ((0, 0), (0, DEGREE_ROWS - owned_count), (0, 0)))
+    packed = aggregate_forward(
+        live_count, block_rows, block_slots, adjacency, fetched, part_deg, node_count
+    )
+    packed = packed.reshape(col_count * (node_count + DEGREE_ROWS), feat_width)
     reduced = lax.psum_scatter(packed, "col", scatter_dimension=0, tiled=True)
     summed = reduced[:node_count]
     degree = reduced[node_count : node_count + owned_count].reshape(node_count)
@@ -216,13 +228,17 @@
     adjoint_panel = lax.all_gather(grad_agg, "col", axis=0, tiled=True)
     weight_pack = exchange_add(weight_pack, steps[0])
     weight_pack, adjoint_panel = lax.optimization_barrier((weight_pack, adjoint_panel))
-    panel_t = adjoint_panel.reshape(panel_blocks, block_size, feat_width).transpose(0, 2, 1)
-    per_slot_t = aggregate_backward(
-        live_count, block_rows, block_slots, blocks[0, 0], panel_t, fetch_total
+    per_slot = aggregate_backward(
+        live_count,
+        block_rows,
+        block_slots,
+        adjacency,
+        adjoint_panel.reshape(panel_blocks, block_size, feat_width),
+        fetch_total,
     )
     weight_pack = exchange_add(weight_pack, steps[1])
-    weight_pack, per_slot_t = lax.optimization_barrier((weight_pack, per_slot_t))
-    per_slot = per_slot_t.transpose(0, 2, 1).reshape(row_count, picks_each, block_size, feat_width)
+    weight_pack, per_slot = lax.optimization_barrier((weight_pack, per_slot))
+    per_slot = per_slot.reshape(row_count, picks_each, block_size, feat_width)
     returned = lax.all_to_all(per_slot, "row", split_axis=0, concat_axis=0, tiled=True)
     weight_pack = exchange_add(weight_pack, steps[2])
     weight_pack, returned = lax.optimization_barrier((weight_pack, returned))

time: 178 us -> 167 us (0.938)
  waiting for transfers between devices: 90 us -> 80.8 us
  local copies, waits for them, and re-layouts: 10.5 us -> 5.46 us
  other arithmetic: 8.39 us -> 12.8 us
  Pallas kernels: 26.9 us -> 23.9 us
    all_to_all x1, waiting for transfers between devices: 11.3 us -> 2.88 us  [on_device(): lax.all_to_all(outgoing, 'row', split_axis=0, concat_axis=0, tiled=True)]
    reduce_sum x0 -> x1, other arithmetic: none -> 6.74 us  [on_device(): jnp.sum(adjacency, axis=2, dtype=jnp.float32)]
    reshape x2 -> x0, local copies, waits for them, and re-layouts: 4.79 us -> none  [the longest x1 2.53 us: on_device(): per_slot_t.transpose(0, 2, 1)]
    pallas_call x1, Pallas kernels: 15.4 us -> 11.8 us  [aggregate_forward(): pl.pallas_call(_forward_kernel, grid_spec=grid_spec, out_shape=jax.ShapeD...]
    concatenate x1 -> x0, other arithmetic: 3.12 us -> none  [on_device(): packed = jnp.concatenate([part_sums, part_deg], axis=1)]
    ppermute x5, waiting for transfers between devices: 34.9 us -> 32.9 us  [exchange_add(): return values + lax.ppermute(values, name, pairs)]
  transfers between devices with their start and end apart: 10 -> 10, of which waited for: 8 -> 8; matrix products, arithmetic and copies ran while one was open for 4% -> 8% of each run, Pallas kernels for 6% -> 7%
where the time goes in v4:
time: 167 us; the launch traced here: 166 us
  waiting for transfers between devices  80.8 us (48%)
  Pallas kernels  23.9 us (14%)
  starting transfers between devices  22 us (13%)
  between operations  14.9 us (9%)
  other arithmetic  12.8 us (8%)
  matrix products  6.36 us (4%)
  local copies, waits for them, and re-layouts  5.46 us (3%)
    ppermute x5, waiting for transfers between devices, exchange_add(): return values + lax.ppermute(values, name, pairs)  32.9 us
    reduce_scatter x1, waiting for transfers between devices, on_device(): reduced = lax.psum_scatter(packed, 'col', scatter_dimension=0, tiled=True)  30.3 us
    pallas_call x1, Pallas kernels, aggregate_backward(): pl.pallas_call(_backward_kernel, grid_spec=grid_spec, out_shape=jax.Shape...  12.1 us
    pallas_call x1, Pallas kernels, aggregate_forward(): pl.pallas_call(_forward_kernel, grid_spec=grid_spec, out_shape=jax.ShapeD...  11.8 us
    all_to_all x1, waiting for transfers between devices, on_device(): lax.all_to_all(per_slot, 'row', split_axis=0, concat_axis=0, tiled=True)  7.96 us
    all_to_all x1, starting transfers between devices, on_device(): lax.all_to_all(wanted, 'row', split_axis=0, concat_axis=0, tiled=True)  7.31 us
    reduce_sum x1, other arithmetic, on_device(): jnp.sum(adjacency, axis=2, dtype=jnp.float32)  6.74 us
    ppermute x5, starting transfers between devices, exchange_add(): return values + lax.ppermute(values, name, pairs)  6.52 us
  transfers between devices with their start and end apart: 10, of which 8 were waited for; matrix products, arithmetic and copies ran while one was open for 8% of the time, Pallas kernels for 7%

profile of v4, /device:TPU:0, one launch (start us, length us, event | category | flops | bytes accessed | tf_op | source)
XLA Modules:
  0.0 166.2 jit_solution(14780127267655445938)
XLA Ops:
  7.2 1.4 copy.17
  8.6 7.3 %all-to-all-start = ((s32[8,1,2]{2,1,0:T(1,128)}), s32[8,1,2]{2,1,0:T(1,128)S(1)}, u32[]{:S(2)}, u32[]{:S(2)}) async-start(s32[8,1,2]{2,1,0:T(1,128)} %copy.17), calls=%async_computation | async-start | bytes 8192 | tf_op jit(solution)/shard_map/all_to_all | solution.py:180
  15.9 1.1 reshape_reshape_squeeze.3
  16.9 5.4 %all-to-all-done = s32[8,1,2]{2,1,0:T(1,128)S(1)} async-done(((s32[8,1,2]{2,1,0:T(1,128)}), s32[8,1,2]{2,1,0:T(1,128)S(1)}, u32[]{:S(2)}, u32[]{:S(2)}) %all-to-all-start) | async-done | bytes 96 | tf_op jit(solution)/shard_map/all_to_all | solution.py:180
  22.8 0.7 reduce.5
  23.9 0.9 copy.18
  24.8 3.5 %all-to-all-start.1 = ((bf16[8,2,128,128]{3,2,1,0:T(8,128)(2,1)}), bf16[8,2,128,128]{3,2,1,0:T(8,128)(2,1)S(1)}, u32[]{:S(2)}, u32[]{:S(2)}) async-start(bf16[8,2,128,128]{3,2,1,0:T(8,128)(2,1)} %bitcast.19), calls=%async_computation.1 | async-start | bytes 1048576 | tf_op jit(solution)/shard_map/all_to_all | solution.py:187
  28.3 0.7 reduce.row_ref
  29.7 1.3 reduce.1.slot_ref
  31.0 6.7 %convert_reduce_fusion = f32[320,128]{1,0:T(8,128)S(1)} fusion(bf16[1,1,320,128,128]{4,3,2,1,0:T(8,128)(2,1)} %param.14), kind=kLoop, calls=%fused_computation | loop fusion | flops 10444800 | bytes 10649600 | tf_op jit(solution)/shard_map/reduce_sum | solution.py:192
  38.0 0.6 pad.4.deg_ref
  38.7 2.9 %all-to-all-done.1 = bf16[8,2,128,128]{3,2,1,0:T(8,128)(2,1)S(1)} async-done(((bf16[8,2,128,128]{3,2,1,0:T(8,128)(2,1)}), bf16[8,2,128,128]{3,2,1,0:T(8,128)(2,1)S(1)}, u32[]{:S(2)}, u32[]{:S(2)}) %all-to-all-start.1) | async-done | bytes 524320 | tf_op jit(solution)/shard_map/all_to_all | solution.py:187
  41.6 0.8 copy-done.2
  42.3 11.8 %shard_map.137 = f32[4,1040,128]{2,1,0:T(8,128)} custom-call(s32[1]{0:T(128)} %bitcast.49.count_ref, s32[320]{0:T(512)} %copy-done.4, s32[320]{0:T(512)} %reduce.1.slot_ref, bf16[320,128,128]{2,1,0:T(8,128)(2,1)} %bitcast.52, bf16[16,128,128]{2,1,0:T(8,128)(2,1)} %bitcast.57, f32[4,16,128]{2,1,0:T(8,128)} %pad.4.deg_ref), custom_call_target="tpu_custom_call" | custom-call | flops 1342177280 | bytes 13139968 | tf_op jit(solution)/shard_map/pallas_call | solution.py:108
  54.5 30.3 %reduce-scatter.2.cloned.1.call-done = f32[1040,128]{1,0:T(8,128)} async-done(((f32[4160,128]{1,0:T(8,128)}), f32[1040,128]{1,0:T(8,128)}) %reduce-scatter.2.cloned.1.call-update) | async-done | bytes 532496 | tf_op jit(solution)/shard_map/reduce_scatter | solution.py:202
  84.8 0.7 fusion.27
  85.5 1.2 fusion.18
  86.8 1.9 %convert_reduce_fusion.1 = (f32[256]{0:T(256)S(1)}, bf16[1024,256]{1,0:T(8,128)(2,1)S(1)}, bf16[1,1024,256]{2,1,0:T(8,128)(2,1)}) fusion(bf16[1,1024,256]{2,1,0:T(8,128)(2,1)S(1)} %copy-done.5, f32[256]{0:T(256)S(1)} %copy-done.6, f32[1024,256]{1,0:T(8,128)S(1)} %fusion.21, bf16[1024,128]{1,0:T(8,128)(2,1)S(1)} %fusion.18, bf16[128,256]{1,0:T(8,128)(2,1)S(1)} %copy-done), kind=kOutput, calls=%fused_computation.29 | convolution fusion | flops 74186496 | bytes 2951168 | tf_op jit(solution)/shard_map/dot_general | solution.py:209
  88.6 1.0 fusion.3
  90.2 2.5 %collective-permute-start = (f32[264,256]{1,0:T(8,128)S(1)}, f32[264,256]{1,0:T(8,128)S(1)}, u32[]{:S(2)}, u32[]{:S(2)}) collective-permute-start(f32[264,256]{1,0:T(8,128)S(1)} %pad_maximum_fusion), channel_id=1, source_target_pairs={{0,16},{4,20},{8,24},{12,28},{16,0},{20,4},{24,8},{28,12},{1,17},{... | collective-permute-start | bytes 811016 | tf_op jit(solution)/shard_map/ppermute | solution.py:164
  92.7 12.3 %collective-permute-done = f32[264,256]{1,0:T(8,128)S(1)} collective-permute-done((f32[264,256]{1,0:T(8,128)S(1)}, f32[264,256]{1,0:T(8,128)S(1)}, u32[]{:S(2)}, u32[]{:S(2)}) %collective-permute-start) | collective-permute-done | bytes 270368 | tf_op jit(solution)/shard_map/ppermute | solution.py:164
  105.1 1.4 all-gather.2.cloned.1.call-done
  106.5 1.5 collective-permute-start.1
  108.0 12.1 %shard_map.138 = f32[16,128,128]{2,1,0:T(8,128)} custom-call(s32[1]{0:T(128)} %bitcast.50.count_ref, s32[320]{0:T(512)} %copy-done.4, s32[320]{0:T(512)} %reduce.1.slot_ref, bf16[320,128,128]{2,1,0:T(8,128)(2,1)} %bitcast.53, bf16[32,128,128]{2,1,0:T(8,128)(2,1)} %bitcast.58), custom_call_target="tpu_custom_call" | custom-call | flops 1342177280 | bytes 12582912 | tf_op jit(solution)/shard_map/pallas_call | solution.py:137
  120.2 4.6 %all-to-all-start.2 = ((f32[8,2,128,128]{3,2,1,0:T(8,128)}), f32[8,2,128,128]{3,2,1,0:T(8,128)S(1)}, u32[]{:S(2)}, u32[]{:S(2)}) async-start(f32[8,2,128,128]{3,2,1,0:T(8,128)} %bitcast.55), calls=%async_computation.3 | async-start | bytes 2097152 | tf_op jit(solution)/shard_map/all_to_all | solution.py:242
  124.7 2.0 %collective-permute-start.2 = (f32[264,256]{1,0:T(8,128)S(1)}, f32[264,256]{1,0:T(8,128)S(1)}, u32[]{:S(2)}, u32[]{:S(2)}) collective-permute-start(f32[264,256]{1,0:T(8,128)S(1)} %add.62), channel_id=1, source_target_pairs={{0,4},{4,0},{8,12},{12,8},{16,20},{20,16},{24,28},{28,24},{1,5},{5... | collective-permute-start | bytes 811016 | tf_op jit(solution)/shard_map/ppermute | solution.py:164
  126.8 14.6 %collective-permute-done.2 = f32[264,256]{1,0:T(8,128)S(1)} collective-permute-done((f32[264,256]{1,0:T(8,128)S(1)}, f32[264,256]{1,0:T(8,128)S(1)}, u32[]{:S(2)}, u32[]{:S(2)}) %collective-permute-start.2) | collective-permute-done | bytes 270368 | tf_op jit(solution)/shard_map/ppermute | solution.py:164
  141.4 8.0 %all-to-all-done.2 = f32[8,2,128,128]{3,2,1,0:T(8,128)S(1)} async-done(((f32[8,2,128,128]{3,2,1,0:T(8,128)}), f32[8,2,128,128]{3,2,1,0:T(8,128)S(1)}, u32[]{:S(2)}, u32[]{:S(2)}) %all-to-all-start.2) | async-done | bytes 1048608 | tf_op jit(solution)/shard_map/all_to_all | solution.py:242
  149.8 6.0 %collective-permute-done.3 = f32[264,256]{1,0:T(8,128)S(1)} collective-permute-done((f32[264,256]{1,0:T(8,128)S(1)}, f32[264,256]{1,0:T(8,128)S(1)}, u32[]{:S(2)}, u32[]{:S(2)}) %collective-permute-start.3) | collective-permute-done | bytes 270368 | tf_op jit(solution)/shard_map/ppermute | solution.py:164
  155.9 1.1 fusion.15
  157.1 1.0 fusion.4
  158.1 0.7 slice_multiply_fusion
  (38 shorter events, 3.6 us)
Async XLA Ops:
  7.2 79.6 %copy-start = (bf16[128,256]{1,0:T(8,128)(2,1)S(1)}, bf16[128,256]{1,0:T(8,128)(2,1)}, u32[]{:S(2)}) copy-start(bf16[128,256]{1,0:T(8,128)(2,1)} %param.12) | copy-start | bytes 196612
  8.6 13.7 %all-to-all-start = ((s32[8,1,2]{2,1,0:T(1,128)}), s32[8,1,2]{2,1,0:T(1,128)S(1)}, u32[]{:S(2)}, u32[]{:S(2)}) async-start(s32[8,1,2]{2,1,0:T(1,128)} %copy.17), calls=%async_computation | async-start | bytes 8192 | tf_op jit(solution)/shard_map/all_to_all | solution.py:180
  24.8 16.8 %all-to-all-start.1 = ((bf16[8,2,128,128]{3,2,1,0:T(8,128)(2,1)}), bf16[8,2,128,128]{3,2,1,0:T(8,128)(2,1)S(1)}, u32[]{:S(2)}, u32[]{:S(2)}) async-start(bf16[8,2,128,128]{3,2,1,0:T(8,128)(2,1)} %bitcast.19), calls=%async_computation.1 | async-start | bytes 1048576 | tf_op jit(solution)/shard_map/all_to_all | solution.py:187
  28.3 56.5 %reduce-scatter.2.cloned.1.call-start = ((), (), s32[]{:S(2)}) async-start(), calls=%async_computation.4 | async-start | bytes 2662400 | tf_op jit(solution)/shard_map/reduce_scatter | solution.py:202
  29.0 12.5 %copy-start.4 = (s32[320]{0:T(512)}, s32[320]{0:T(512)S(1)}, u32[]{:S(2)}) copy-start(s32[320]{0:T(512)S(1)} %reduce.row_ref) | copy-start | bytes 3844
  31.0 23.2 %copy-start.1 = (bf16[1,1024,128]{2,1,0:T(8,128)(2,1)S(1)}, bf16[1,1024,128]{2,1,0:T(8,128)(2,1)}, u32[]{:S(2)}) copy-start(bf16[1,1024,128]{2,1,0:T(8,128)(2,1)} %param.10) | copy-start | bytes 786436
  31.0 23.2 %copy-start.3 = (bf16[128,256]{1,0:T(8,128)(2,1)S(1)}, bf16[128,256]{1,0:T(8,128)(2,1)}, u32[]{:S(2)}) copy-start(bf16[128,256]{1,0:T(8,128)(2,1)} %param.11) | copy-start | bytes 196612
  37.7 49.0 %copy-start.5 = (bf16[1,1024,256]{2,1,0:T(8,128)(2,1)S(1)}, bf16[1,1024,256]{2,1,0:T(8,128)(2,1)}, u32[]{:S(2)}) copy-start(bf16[1,1024,256]{2,1,0:T(8,128)(2,1)} %param.19) | copy-start | bytes 1572868
  37.8 49.0 %copy-start.6 = (f32[256]{0:T(256)S(1)}, f32[256]{0:T(256)}, u32[]{:S(2)}) copy-start(f32[256]{0:T(256)} %param.13) | copy-start | bytes 3076
  41.5 0.8 copy-start.2
  54.1 52.4 %all-gather.2.cloned.1.call-start = ((), (), s32[]{:S(2)}) async-start(), calls=%async_computation.5 | async-start | bytes 1310720 | tf_op jit(solution)/shard_map/all_gather | solution.py:228
  90.2 14.8 %collective-permute-start = (f32[264,256]{1,0:T(8,128)S(1)}, f32[264,256]{1,0:T(8,128)S(1)}, u32[]{:S(2)}, u32[]{:S(2)}) collective-permute-start(f32[264,256]{1,0:T(8,128)S(1)} %pad_maximum_fusion), channel_id=1, source_target_pairs={{0,16},{4,20},{8,24},{12,28},{16,0},{20,4},{24,8},{28,12},{1,17},{... | collective-permute-start | bytes 811016 | tf_op jit(solution)/shard_map/ppermute | solution.py:164
  106.5 13.6 %collective-permute-start.1 = (f32[264,256]{1,0:T(8,128)S(1)}, f32[264,256]{1,0:T(8,128)S(1)}, u32[]{:S(2)}, u32[]{:S(2)}) collective-permute-start(f32[264,256]{1,0:T(8,128)S(1)} %fusion.31), channel_id=1, source_target_pairs={{0,8},{4,12},{8,0},{12,4},{16,24},{20,28},{24,16},{28,20},{1,9},{5... | collective-permute-start | bytes 811016 | tf_op jit(solution)/shard_map/ppermute | solution.py:164
  120.2 29.2 %all-to-all-start.2 = ((f32[8,2,128,128]{3,2,1,0:T(8,128)}), f32[8,2,128,128]{3,2,1,0:T(8,128)S(1)}, u32[]{:S(2)}, u32[]{:S(2)}) async-start(f32[8,2,128,128]{3,2,1,0:T(8,128)} %bitcast.55), calls=%async_computation.3 | async-start | bytes 2097152 | tf_op jit(solution)/shard_map/all_to_all | solution.py:242
  124.7 16.6 %collective-permute-start.2 = (f32[264,256]{1,0:T(8,128)S(1)}, f32[264,256]{1,0:T(8,128)S(1)}, u32[]{:S(2)}, u32[]{:S(2)}) collective-permute-start(f32[264,256]{1,0:T(8,128)S(1)} %add.62), channel_id=1, source_target_pairs={{0,4},{4,0},{8,12},{12,8},{16,20},{20,16},{24,28},{28,24},{1,5},{5... | collective-permute-start | bytes 811016 | tf_op jit(solution)/shard_map/ppermute | solution.py:164
  149.3 6.5 %collective-permute-start.3 = (f32[264,256]{1,0:T(8,128)S(1)}, f32[264,256]{1,0:T(8,128)S(1)}, u32[]{:S(2)}, u32[]{:S(2)}) collective-permute-start(f32[264,256]{1,0:T(8,128)S(1)} %add.63), channel_id=1, source_target_pairs={{0,2},{1,3},{2,0},{3,1},{4,6},{5,7},{6,4},{7,5},{8,10},{9,11},{10,... | collective-permute-start | bytes 811016 | tf_op jit(solution)/shard_map/ppermute | solution.py:164
  155.8 2.2 %collective-permute-start.4 = (f32[264,256]{1,0:T(8,128)S(1)}, f32[264,256]{1,0:T(8,128)S(1)}, u32[]{:S(2)}, u32[]{:S(2)}) collective-permute-start(f32[264,256]{1,0:T(8,128)S(1)} %add.65), channel_id=1, source_target_pairs={{0,1},{1,0},{2,3},{3,2},{4,5},{5,4},{6,7},{7,6},{8,9},{9,8},{10,11... | collective-permute-start | bytes 811016 | tf_op jit(solution)/shard_map/ppermute | solution.py:164
Sparse Core Ops, SparseCore 0:
  54.3 30.4 reduce-scatter.1
  89.8 16.6 all-gather.1

commit v5 on v4

--- a/solution.py
+++ b/solution.py
@@ -63,10 +63,12 @@
             out_ref[r // owned, pl.ds(at, bs), :] += jnp.where(live, prod, 0.0)
 
 
-def _backward_kernel(count_ref, row_ref, slot_ref, blk_ref, grad_ref, out_ref, gt_ref, acc_ref):
-    g = pl.program_id(0)
-
-    @pl.when(g == 0)
+def _backward_kernel(
+    first, count_ref, row_ref, slot_ref, blk_ref, grad_ref, prev_ref, out_ref, gt_ref, acc_ref
+):
+    g = pl.program_id(0) + first
+
+    @pl.when(pl.program_id(0) == 0)
     def _():
         for r in range(grad_ref.shape[0]):
             gt_ref[r] = grad_ref[r].T
@@ -84,10 +86,10 @@
             prod = jnp.dot(gt_ref[r], blk_ref[j], preferred_element_type=jnp.float32)
             acc_ref[s] += jnp.where(live, prod, 0.0)
 
-    @pl.when(g == pl.num_programs(0) - 1)
+    @pl.when(pl.program_id(0) == pl.num_programs(0) - 1)
     def _():
         for s in range(out_ref.shape[0]):
-            out_ref[s] = acc_ref[s].T
+            out_ref[s] = acc_ref[s].T + prev_ref[s]
 
 
 def aggregate_forward(counts, rows, slots, blocks, fetched, degree_rows, node_count):
@@ -118,15 +120,21 @@
     )(counts, rows, slots, blocks, fetched, degree_rows)
 
 
-def aggregate_backward(counts, rows, slots, blocks, grad_panel, fetch_total):
+def aggregate_backward(counts, rows, slots, blocks, grad_panel, previous, first, last):
     slot_total, bs, _ = blocks.shape
     panel_blocks, _, width = grad_panel.shape
+    fetch_total = previous.shape[0]
+
+    def block_at(g, c, r, s):
+        return (_live_group(g + first, c), 0, 0)
+
     grid_spec = pltpu.PrefetchScalarGridSpec(
         num_scalar_prefetch=3,
-        grid=(slot_total // GROUP,),
+        grid=(last - first,),
         in_specs=[
-            pl.BlockSpec((GROUP, bs, bs), lambda g, c, r, s: (_live_group(g, c), 0, 0)),
+            pl.BlockSpec((GROUP, bs, bs), block_at),
             pl.BlockSpec((panel_blocks, bs, width), lambda g, c, r, s: (0, 0, 0)),
+            pl.BlockSpec((fetch_total, bs, width), lambda g, c, r, s: (0, 0, 0)),
         ],
         out_specs=pl.BlockSpec((fetch_total, bs, width), lambda g, c, r, s: (0, 0, 0)),
         scratch_shapes=[
@@ -134,17 +142,18 @@
             pltpu.VMEM((fetch_total, width, bs), jnp.float32),
         ],
     )
+    share = (last - first) * GROUP
     return pl.pallas_call(
-        _backward_kernel,
+        functools.partial(_backward_kernel, first),
         grid_spec=grid_spec,
         out_shape=jax.ShapeDtypeStruct((fetch_total, bs, width), jnp.float32),
         compiler_params=pltpu.CompilerParams(dimension_semantics=("arbitrary",)),
         cost_estimate=pl.CostEstimate(
-            flops=2 * slot_total * bs * bs * width,
-            bytes_accessed=blocks.size * 2 + grad_panel.size * 2 + fetch_total * bs * width * 4,
+            flops=2 * share * bs * bs * width,
+            bytes_accessed=share * bs * bs * 2 + grad_panel.size * 2 + fetch_total * bs * width * 8,
             transcendentals=0,
         ),
-    )(counts, rows, slots, blocks, grad_panel)
+    )(counts, rows, slots, blocks, grad_panel, previous)
 
 
 def exchange_steps(axes):
@@ -220,6 +229,7 @@
         [local_self, local_neigh, jnp.broadcast_to(local_bias[None], (8, hid))], axis=0
     )
     steps = exchange_steps(("col", "row"))
+    cross_step = [step for step in steps if step[0] == "col"][0]
     grad_agg = (
         jnp.einsum("nh,dh->nd", grad_round, w_neigh, preferred_element_type=jnp.float32)
         / divisor[:, None]
@@ -228,19 +238,23 @@
     adjoint_panel = lax.all_gather(grad_agg, "col", axis=0, tiled=True)
     weight_pack = exchange_add(weight_pack, steps[0])
     weight_pack, adjoint_panel = lax.optimization_barrier((weight_pack, adjoint_panel))
+    panel = adjoint_panel.reshape(panel_blocks, block_size, feat_width)
+    groups = adjacency.shape[0] // GROUP
+    half = groups // 2
+    per_slot = jnp.zeros((fetch_total, block_size, feat_width), jnp.float32)
     per_slot = aggregate_backward(
-        live_count,
-        block_rows,
-        block_slots,
-        adjacency,
-        adjoint_panel.reshape(panel_blocks, block_size, feat_width),
-        fetch_total,
+        live_count, block_rows, block_slots, adjacency, panel, per_slot, 0, half
     )
     weight_pack = exchange_add(weight_pack, steps[1])
+    weight_pack, per_slot = lax.optimization_barrier((weight_pack, per_slot))
+    per_slot = aggregate_backward(
+        live_count, block_rows, block_slots, adjacency, panel, per_slot, half, groups
+    )
+    weight_pack = exchange_add(weight_pack, steps[2])
     weight_pack, per_slot = lax.optimization_barrier((weight_pack, per_slot))
     per_slot = per_slot.reshape(row_count, picks_each, block_size, feat_width)
     returned = lax.all_to_all(per_slot, "row", split_axis=0, concat_axis=0, tiled=True)
-    weight_pack = exchange_add(weight_pack, steps[2])
+    weight_pack = exchange_add(weight_pack, cross_step)
     weight_pack, returned = lax.optimization_barrier((weight_pack, returned))
     incoming = group_rows(
         asked_for.reshape(-1),
@@ -252,7 +266,8 @@
         jnp.einsum("nh,dh->nd", grad_round, w_self, preferred_element_type=jnp.float32) + incoming
     )
     for step in steps[3:]:
-        weight_pack = exchange_add(weight_pack, step)
+        if step != cross_step:
+            weight_pack = exchange_add(weight_pack, step)
     factor = 1.0 / math.sqrt(node_count * row_count * col_count)
     grad_self = weight_pack[:feat_width] * factor
     grad_neigh = weight_pack[feat_width : 2 * feat_width] * factor

time: 167 us -> 166 us (level)
  Pallas kernels: 23.9 us -> 28.2 us
  waiting for transfers between devices: 80.8 us -> 77.3 us
    ppermute x5, waiting for transfers between devices: 32.9 us -> 19.5 us  [exchange_add(): return values + lax.ppermute(values, name, pairs)]
    all_to_all x1, waiting for transfers between devices: 7.96 us -> 17.8 us  [on_device(): lax.all_to_all(per_slot, 'row', split_axis=0, concat_axis=0, tiled=True)]
    pallas_call x1 -> x2, Pallas kernels: 12.1 us -> 16.4 us  [aggregate_backward(): pl.pallas_call(functools.partial(_backward_kernel, first), grid_spec=grid...]
  transfers between devices with their start and end apart: 10 -> 10, of which waited for: 8 -> 7; matrix products, arithmetic and copies ran while one was open for 8% -> 9% of each run, Pallas kernels for 7% -> 10%
where the time goes in v5:
time: 166 us; the launch traced here: 167 us
  waiting for transfers between devices  77.3 us (47%)
  Pallas kernels  28.2 us (17%)
  starting transfers between devices  20.6 us (12%)
  between operations  14.9 us (9%)
  other arithmetic  12.7 us (8%)
  local copies, waits for them, and re-layouts  6.56 us (4%)
  matrix products  6.36 us (4%)
    reduce_scatter x1, waiting for transfers between devices, on_device(): reduced = lax.psum_scatter(packed, 'col', scatter_dimension=0, tiled=True)  30.3 us
    ppermute x5, waiting for transfers between devices, exchange_add(): return values + lax.ppermute(values, name, pairs)  19.5 us
    all_to_all x1, waiting for transfers between devices, on_device(): lax.all_to_all(per_slot, 'row', split_axis=0, concat_axis=0, tiled=True)  17.8 us
    pallas_call x2, Pallas kernels, aggregate_backward(): pl.pallas_call(functools.partial(_backward_kernel, first), grid_spec=grid...  16.4 us
    pallas_call x1, Pallas kernels, aggregate_forward(): pl.pallas_call(_forward_kernel, grid_spec=grid_spec, out_shape=jax.ShapeD...  11.8 us
    all_to_all x1, starting transfers between devices, on_device(): lax.all_to_all(wanted, 'row', split_axis=0, concat_axis=0, tiled=True)  7.31 us
    reduce_sum x1, other arithmetic, on_device(): jnp.sum(adjacency, axis=2, dtype=jnp.float32)  6.74 us
    all_to_all x1, waiting for transfers between devices, on_device(): lax.all_to_all(wanted, 'row', split_axis=0, concat_axis=0, tiled=True)  5.35 us
  transfers between devices with their start and end apart: 10, of which 7 were waited for; matrix products, arithmetic and copies ran while one was open for 9% of the time, Pallas kernels for 10%

profile of v5, /device:TPU:0, one launch (start us, length us, event | category | flops | bytes accessed | tf_op | source)
XLA Modules:
  0.0 166.6 jit_solution(10788926208088493095)
XLA Ops:
  7.2 1.4 copy.17
  8.6 7.3 %all-to-all-start = ((s32[8,1,2]{2,1,0:T(1,128)}), s32[8,1,2]{2,1,0:T(1,128)S(1)}, u32[]{:S(2)}, u32[]{:S(2)}) async-start(s32[8,1,2]{2,1,0:T(1,128)} %copy.17), calls=%async_computation | async-start | bytes 8192 | tf_op jit(solution)/shard_map/all_to_all | solution.py:189
  15.9 1.1 reshape_reshape_squeeze.3
  16.9 5.4 %all-to-all-done = s32[8,1,2]{2,1,0:T(1,128)S(1)} async-done(((s32[8,1,2]{2,1,0:T(1,128)}), s32[8,1,2]{2,1,0:T(1,128)S(1)}, u32[]{:S(2)}, u32[]{:S(2)}) %all-to-all-start) | async-done | bytes 96 | tf_op jit(solution)/shard_map/all_to_all | solution.py:189
  22.8 0.7 reduce.5
  23.9 0.9 copy.18
  24.8 3.5 %all-to-all-start.1 = ((bf16[8,2,128,128]{3,2,1,0:T(8,128)(2,1)}), bf16[8,2,128,128]{3,2,1,0:T(8,128)(2,1)S(1)}, u32[]{:S(2)}, u32[]{:S(2)}) async-start(bf16[8,2,128,128]{3,2,1,0:T(8,128)(2,1)} %bitcast.19), calls=%async_computation.1 | async-start | bytes 1048576 | tf_op jit(solution)/shard_map/all_to_all | solution.py:196
  29.0 0.7 reduce.row_ref
  29.7 1.2 reduce.1.slot_ref
  31.0 6.7 %convert_reduce_fusion = f32[320,128]{1,0:T(8,128)S(1)} fusion(bf16[1,1,320,128,128]{4,3,2,1,0:T(8,128)(2,1)} %param.14), kind=kLoop, calls=%fused_computation | loop fusion | flops 10444800 | bytes 10649600 | tf_op jit(solution)/shard_map/reduce_sum | solution.py:201
  38.6 2.9 %all-to-all-done.1 = bf16[8,2,128,128]{3,2,1,0:T(8,128)(2,1)S(1)} async-done(((bf16[8,2,128,128]{3,2,1,0:T(8,128)(2,1)}), bf16[8,2,128,128]{3,2,1,0:T(8,128)(2,1)S(1)}, u32[]{:S(2)}, u32[]{:S(2)}) %all-to-all-start.1) | async-done | bytes 524320 | tf_op jit(solution)/shard_map/all_to_all | solution.py:196
  41.6 0.8 copy-done.2
  42.3 11.8 %shard_map.137 = f32[4,1040,128]{2,1,0:T(8,128)} custom-call(s32[1]{0:T(128)} %bitcast.49.count_ref, s32[320]{0:T(512)} %copy-done.4, s32[320]{0:T(512)} %reduce.1.slot_ref, bf16[320,128,128]{2,1,0:T(8,128)(2,1)} %bitcast.53, bf16[16,128,128]{2,1,0:T(8,128)(2,1)} %bitcast.61, f32[4,16,128]{2,1,0:T(8,128)} %pad.4.deg_ref), custom_call_target="tpu_custom_call" | custom-call | flops 1342177280 | bytes 13139968 | tf_op jit(solution)/shard_map/pallas_call | solution.py:110
  54.5 30.3 %reduce-scatter.2.cloned.1.call-done = f32[1040,128]{1,0:T(8,128)} async-done(((f32[4160,128]{1,0:T(8,128)}), f32[1040,128]{1,0:T(8,128)}) %reduce-scatter.2.cloned.1.call-update) | async-done | bytes 532496 | tf_op jit(solution)/shard_map/reduce_scatter | solution.py:211
  84.8 0.7 fusion.27
  85.4 1.2 fusion.18
  86.7 1.9 %convert_reduce_fusion.1 = (f32[256]{0:T(256)S(1)}, bf16[1024,256]{1,0:T(8,128)(2,1)S(1)}, bf16[1,1024,256]{2,1,0:T(8,128)(2,1)}) fusion(bf16[1,1024,256]{2,1,0:T(8,128)(2,1)S(1)} %copy-done.5, f32[256]{0:T(256)S(1)} %copy-done.6, f32[1024,256]{1,0:T(8,128)S(1)} %fusion.21, bf16[1024,128]{1,0:T(8,128)(2,1)S(1)} %fusion.18, bf16[128,256]{1,0:T(8,128)(2,1)S(1)} %copy-done), kind=kOutput, calls=%fused_computation.29 | convolution fusion | flops 74186496 | bytes 2951168 | tf_op jit(solution)/shard_map/dot_general | solution.py:218
  88.6 1.0 fusion.3
  90.2 2.5 %collective-permute-start = (f32[264,256]{1,0:T(8,128)S(1)}, f32[264,256]{1,0:T(8,128)S(1)}, u32[]{:S(2)}, u32[]{:S(2)}) collective-permute-start(f32[264,256]{1,0:T(8,128)S(1)} %pad_maximum_fusion), channel_id=1, source_target_pairs={{0,16},{4,20},{8,24},{12,28},{16,0},{20,4},{24,8},{28,12},{1,17},{... | collective-permute-start | bytes 811016 | tf_op jit(solution)/shard_map/ppermute | solution.py:173
  92.7 12.3 %collective-permute-done = f32[264,256]{1,0:T(8,128)S(1)} collective-permute-done((f32[264,256]{1,0:T(8,128)S(1)}, f32[264,256]{1,0:T(8,128)S(1)}, u32[]{:S(2)}, u32[]{:S(2)}) %collective-permute-start) | collective-permute-done | bytes 270368 | tf_op jit(solution)/shard_map/ppermute | solution.py:173
  105.1 1.4 all-gather.2.cloned.1.call-done
  106.5 1.5 collective-permute-start.1
  107.9 1.1 broadcast_in_dim.38.prev_ref
  109.0 8.2 %shard_map.138.prev_ref = f32[16,128,128]{2,1,0:T(8,128)} custom-call(s32[1]{0:T(128)} %bitcast.50.count_ref, s32[320]{0:T(512)} %copy-done.4, s32[320]{0:T(512)} %reduce.1.slot_ref, bf16[320,128,128]{2,1,0:T(8,128)(2,1)} %bitcast.54, bf16[32,128,128]{2,1,0:T(8,128)(2,1)} %bitcast.57, f32[16,128,128]{2,1,0:T(8,128)} %broadcast_in_dim.38.prev_ref), custom_call_target="tpu_custom_call" | custom-call | flops 671088640 | bytes 8388608 | tf_op jit(solution)/shard_map/pallas_call | solution.py:146
  117.8 8.2 %shard_map.139 = f32[16,128,128]{2,1,0:T(8,128)} custom-call(s32[1]{0:T(128)} %bitcast.51.count_ref, s32[320]{0:T(512)} %copy-done.4, s32[320]{0:T(512)} %reduce.1.slot_ref, bf16[320,128,128]{2,1,0:T(8,128)(2,1)} %bitcast.55, bf16[32,128,128]{2,1,0:T(8,128)(2,1)} %bitcast.58, f32[16,128,128]{2,1,0:T(8,128)} %shard_map.138.prev_ref), custom_call_target="tpu_custom_call" | custom-call | flops 671088640 | bytes 8388608 | tf_op jit(solution)/shard_map/pallas_call | solution.py:146
  126.0 4.4 %all-to-all-start.2 = ((f32[8,2,128,128]{3,2,1,0:T(8,128)}), f32[8,2,128,128]{3,2,1,0:T(8,128)S(1)}, u32[]{:S(2)}, u32[]{:S(2)}) async-start(f32[8,2,128,128]{3,2,1,0:T(8,128)} %bitcast.59), calls=%async_computation.3 | async-start | bytes 2097152 | tf_op jit(solution)/shard_map/all_to_all | solution.py:256
  130.4 0.9 collective-permute-start.3
  131.3 7.1 %collective-permute-done.3 = f32[264,256]{1,0:T(8,128)S(1)} collective-permute-done((f32[264,256]{1,0:T(8,128)S(1)}, f32[264,256]{1,0:T(8,128)S(1)}, u32[]{:S(2)}, u32[]{:S(2)}) %collective-permute-start.3) | collective-permute-done | bytes 270368 | tf_op jit(solution)/shard_map/ppermute | solution.py:173
  138.4 17.8 %all-to-all-done.2 = f32[8,2,128,128]{3,2,1,0:T(8,128)S(1)} async-done(((f32[8,2,128,128]{3,2,1,0:T(8,128)}), f32[8,2,128,128]{3,2,1,0:T(8,128)S(1)}, u32[]{:S(2)}, u32[]{:S(2)}) %all-to-all-start.2) | async-done | bytes 1048608 | tf_op jit(solution)/shard_map/all_to_all | solution.py:256
  156.2 1.1 fusion.15
  157.4 1.0 fusion.4
  158.4 0.7 slice_multiply_fusion
  (40 shorter events, 4.1 us)
Async XLA Ops:
  7.2 79.5 %copy-start = (bf16[128,256]{1,0:T(8,128)(2,1)S(1)}, bf16[128,256]{1,0:T(8,128)(2,1)}, u32[]{:S(2)}) copy-start(bf16[128,256]{1,0:T(8,128)(2,1)} %param.12) | copy-start | bytes 196612
  8.6 13.7 %all-to-all-start = ((s32[8,1,2]{2,1,0:T(1,128)}), s32[8,1,2]{2,1,0:T(1,128)S(1)}, u32[]{:S(2)}, u32[]{:S(2)}) async-start(s32[8,1,2]{2,1,0:T(1,128)} %copy.17), calls=%async_computation | async-start | bytes 8192 | tf_op jit(solution)/shard_map/all_to_all | solution.py:189
  24.8 16.8 %all-to-all-start.1 = ((bf16[8,2,128,128]{3,2,1,0:T(8,128)(2,1)}), bf16[8,2,128,128]{3,2,1,0:T(8,128)(2,1)S(1)}, u32[]{:S(2)}, u32[]{:S(2)}) async-start(bf16[8,2,128,128]{3,2,1,0:T(8,128)(2,1)} %bitcast.19), calls=%async_computation.1 | async-start | bytes 1048576 | tf_op jit(solution)/shard_map/all_to_all | solution.py:196
  28.3 56.5 %reduce-scatter.2.cloned.1.call-start = ((), (), s32[]{:S(2)}) async-start(), calls=%async_computation.4 | async-start | bytes 2662400 | tf_op jit(solution)/shard_map/reduce_scatter | solution.py:211
  29.7 11.9 %copy-start.4 = (s32[320]{0:T(512)}, s32[320]{0:T(512)S(1)}, u32[]{:S(2)}) copy-start(s32[320]{0:T(512)S(1)} %reduce.row_ref) | copy-start | bytes 3844
  30.9 23.2 %copy-start.1 = (bf16[1,1024,128]{2,1,0:T(8,128)(2,1)S(1)}, bf16[1,1024,128]{2,1,0:T(8,128)(2,1)}, u32[]{:S(2)}) copy-start(bf16[1,1024,128]{2,1,0:T(8,128)(2,1)} %param.10) | copy-start | bytes 786436
  30.9 23.2 %copy-start.3 = (bf16[128,256]{1,0:T(8,128)(2,1)S(1)}, bf16[128,256]{1,0:T(8,128)(2,1)}, u32[]{:S(2)}) copy-start(bf16[128,256]{1,0:T(8,128)(2,1)} %param.11) | copy-start | bytes 196612
  37.7 49.0 %copy-start.5 = (bf16[1,1024,256]{2,1,0:T(8,128)(2,1)S(1)}, bf16[1,1024,256]{2,1,0:T(8,128)(2,1)}, u32[]{:S(2)}) copy-start(bf16[1,1024,256]{2,1,0:T(8,128)(2,1)} %param.19) | copy-start | bytes 1572868
  37.7 49.0 %copy-start.6 = (f32[256]{0:T(256)S(1)}, f32[256]{0:T(256)}, u32[]{:S(2)}) copy-start(f32[256]{0:T(256)} %param.13) | copy-start | bytes 3076
  41.5 0.8 copy-start.2
  54.1 52.3 %all-gather.2.cloned.1.call-start = ((), (), s32[]{:S(2)}) async-start(), calls=%async_computation.5 | async-start | bytes 1310720 | tf_op jit(solution)/shard_map/all_gather | solution.py:238
  90.2 14.8 %collective-permute-start = (f32[264,256]{1,0:T(8,128)S(1)}, f32[264,256]{1,0:T(8,128)S(1)}, u32[]{:S(2)}, u32[]{:S(2)}) collective-permute-start(f32[264,256]{1,0:T(8,128)S(1)} %pad_maximum_fusion), channel_id=1, source_target_pairs={{0,16},{4,20},{8,24},{12,28},{16,0},{20,4},{24,8},{28,12},{1,17},{... | collective-permute-start | bytes 811016 | tf_op jit(solution)/shard_map/ppermute | solution.py:173
  106.5 10.8 %collective-permute-start.1 = (f32[264,256]{1,0:T(8,128)S(1)}, f32[264,256]{1,0:T(8,128)S(1)}, u32[]{:S(2)}, u32[]{:S(2)}) collective-permute-start(f32[264,256]{1,0:T(8,128)S(1)} %fusion.31), channel_id=1, source_target_pairs={{0,8},{4,12},{8,0},{12,4},{16,24},{20,28},{24,16},{28,20},{1,9},{5... | collective-permute-start | bytes 811016 | tf_op jit(solution)/shard_map/ppermute | solution.py:173
  117.3 8.6 %collective-permute-start.2 = (f32[264,256]{1,0:T(8,128)S(1)}, f32[264,256]{1,0:T(8,128)S(1)}, u32[]{:S(2)}, u32[]{:S(2)}) collective-permute-start(f32[264,256]{1,0:T(8,128)S(1)} %add.62), channel_id=1, source_target_pairs={{0,4},{4,0},{8,12},{12,8},{16,20},{20,16},{24,28},{28,24},{1,5},{5... | collective-permute-start | bytes 811016 | tf_op jit(solution)/shard_map/ppermute | solution.py:173
  126.0 30.2 %all-to-all-start.2 = ((f32[8,2,128,128]{3,2,1,0:T(8,128)}), f32[8,2,128,128]{3,2,1,0:T(8,128)S(1)}, u32[]{:S(2)}, u32[]{:S(2)}) async-start(f32[8,2,128,128]{3,2,1,0:T(8,128)} %bitcast.59), calls=%async_computation.3 | async-start | bytes 2097152 | tf_op jit(solution)/shard_map/all_to_all | solution.py:256
  130.4 8.0 %collective-permute-start.3 = (f32[264,256]{1,0:T(8,128)S(1)}, f32[264,256]{1,0:T(8,128)S(1)}, u32[]{:S(2)}, u32[]{:S(2)}) collective-permute-start(f32[264,256]{1,0:T(8,128)S(1)} %add.63), channel_id=1, source_target_pairs={{0,2},{1,3},{2,0},{3,1},{4,6},{5,7},{6,4},{7,5},{8,10},{9,11},{10,... | collective-permute-start | bytes 811016 | tf_op jit(solution)/shard_map/ppermute | solution.py:173
  156.2 2.2 %collective-permute-start.4 = (f32[264,256]{1,0:T(8,128)S(1)}, f32[264,256]{1,0:T(8,128)S(1)}, u32[]{:S(2)}, u32[]{:S(2)}) collective-permute-start(f32[264,256]{1,0:T(8,128)S(1)} %add.64), channel_id=1, source_target_pairs={{0,1},{1,0},{2,3},{3,2},{4,5},{5,4},{6,7},{7,6},{8,9},{9,8},{10,11... | collective-permute-start | bytes 811016 | tf_op jit(solution)/shard_map/ppermute | solution.py:173
Sparse Core Ops, SparseCore 0:
  54.3 30.4 reduce-scatter.1
  89.7 16.6 all-gather.1
